TPU v7x, 512 devices: a whole 4x4x16 slice. The times are simulated.
512 devices in a mesh: ctx: 64 (over z, y_hi, core), chan: 8 (over x, y_lo).
Axes of the slice: x: 4, y: 4 (y_hi: 2, y_lo: 2; y = y_hi * 2 + y_lo), z: 16, core: 2. Of those that a mesh axis runs over, the one named last changes fastest.
Arguments:
- query_pol: bfloat16 [8192, 8192], P('chan', 'ctx'), may hold values from -6 to 6
- keys_pol: bfloat16 [8192, 8192], P('chan', 'ctx'), may hold values from -6 to 6
- value_pol: bfloat16 [8192, 8192], P('chan', 'ctx'), may hold values from -6 to 6
- filter_pol: float32 [4, 8192], P(None, 'ctx'), may hold values from -1.2 to 1.2
- skip_pol: float32 [8192], P('chan'), may hold values from -4 to 4
- query_ref: bfloat16 [8192, 8192], P('chan', 'ctx'), may hold values from -6 to 6
- keys_ref: bfloat16 [8192, 8192], P('chan', 'ctx'), may hold values from -6 to 6
- value_ref: bfloat16 [8192, 8192], P('chan', 'ctx'), may hold values from -6 to 6
- filter_ref: float32 [4, 8192], P(None, 'ctx'), may hold values from -1.2 to 1.2
- skip_ref: float32 [8192], P('chan'), may hold values from -4 to 4
- grad_out: bfloat16 [8192, 8192], P('chan', 'ctx'), may hold values from -0.75 to 0.75
Outputs:
- out_pol: bfloat16 [8192, 8192], P('chan', 'ctx')
- out_ref: bfloat16 [8192, 8192], P('chan', 'ctx')
- grad_query: bfloat16 [8192, 8192], P('chan', 'ctx')
- grad_keys: bfloat16 [8192, 8192], P('chan', 'ctx')
- grad_value: bfloat16 [8192, 8192], P('chan', 'ctx')
- grad_filter: float32 [4, 8192], P(None, 'ctx')
All inputs are finite; a program needn't handle non-finite values.
Results may differ from a plain program's by a relative error of at most 0.003.
Values sent between devices are 32-bit elements; how exact they have to be, the bound alone decides.
No kernel may reach another device: no remote copies, remote signals or barrier semaphores. Data moves between devices by JAX's collectives and lax.ppermute only.
A program may use at most 64 MiB of HBM per device.

v0:
```python
import math

import jax
import jax.numpy as jnp
import numpy as np
from jax import lax
from jax.sharding import PartitionSpec as P

PREC = lax.Precision.HIGH
LANES = 128


def dft_tables(length):
    full = 2 * length
    width = LANES
    outer = full // width
    used = length // width
    a = np.arange(outer)
    b = np.arange(width)
    turn_a = 2.0 * math.pi * ((a[:, None] * a[None, :]) % outer) / outer
    turn_t = 2.0 * math.pi * ((a[:, None] * b[None, :]) % full) / full
    turn_b = 2.0 * math.pi * ((b[:, None] * b[None, :]) % width) / width
    ca, sa = np.cos(turn_a), np.sin(turn_a)
    ct, st = np.cos(turn_t), np.sin(turn_t)
    cb, sb = np.cos(turn_b), np.sin(turn_b)
    fwd_a = np.stack([ca[:, :used], -sa[:, :used]])
    fwd_b = np.block([[cb, -sb], [sb, cb]])
    inv_b = np.block([[cb, sb], [-sb, cb]])
    inv_a = np.stack([ca[:, :used], -sa[:, :used]]) / full
    f32 = lambda t: jnp.asarray(t.astype(np.float32))
    return dict(
        fwd_a=f32(fwd_a), fwd_b=f32(fwd_b), inv_b=f32(inv_b), inv_a=f32(inv_a),
        ct=f32(ct), st=f32(st), outer=outer, used=used, width=width,
    )


def forward_dft(x, tab):
    rows = x.shape[0]
    xa = x.reshape(rows, tab["used"], tab["width"])
    y = jnp.einsum("rab,cka->rckb", xa, tab["fwd_a"], precision=PREC)
    yr, yi = y[:, 0], y[:, 1]
    ct, st = tab["ct"], tab["st"]
    zr = yr * ct + yi * st
    zi = yi * ct - yr * st
    z = jnp.concatenate([zr, zi], axis=-1)
    return jnp.einsum("rkb,bm->rkm", z, tab["fwd_b"], precision=PREC)


def inverse_dft(p, tab):
    rows = p.shape[0]
    width = tab["width"]
    q = jnp.einsum("rkb,bm->rkm", p, tab["inv_b"], precision=PREC)
    qr, qi = q[..., :width], q[..., width:]
    ct, st = tab["ct"], tab["st"]
    q2 = jnp.stack([qr * ct - qi * st, qr * st + qi * ct], axis=1)
    y = jnp.einsum("rckb,cka->rab", q2, tab["inv_a"], precision=PREC)
    return y.reshape(rows, tab["used"] * width)


def cmul(x, h, conj_h, width):
    xr, xi = x[..., :width], x[..., width:]
    hr, hi = h[..., :width], h[..., width:]
    if conj_h:
        return jnp.concatenate([xr * hr + xi * hi, xi * hr - xr * hi], axis=-1)
    return jnp.concatenate([xr * hr - xi * hi, xr * hi + xi * hr], axis=-1)


def local(
    query_pol,
    keys_pol,
    value_pol,
    filter_pol,
    skip_pol,
    query_ref,
    keys_ref,
    value_ref,
    filter_ref,
    skip_ref,
    grad_out,
):
    chan_rows, span = query_pol.shape
    group_count = filter_pol.shape[0]
    gated_pol = keys_pol.astype(jnp.float32) * value_pol.astype(jnp.float32)
    gated_ref = keys_ref.astype(jnp.float32) * value_ref.astype(jnp.float32)
    out_grad = grad_out.astype(jnp.float32)
    grad_sum = out_grad * query_pol.astype(jnp.float32)

    shards = lax.axis_size("ctx")
    own_rows = chan_rows // shards
    fields = jnp.stack([gated_pol, gated_ref, grad_sum])
    fields = fields.reshape(3, shards, own_rows, span).transpose(1, 0, 2, 3)
    fields = fields.reshape(shards, 3 * own_rows, span)
    filt = jnp.concatenate([filter_pol, filter_ref], axis=0)
    filt_rows = filt.shape[0]
    send = jnp.concatenate([fields, jnp.broadcast_to(filt[None], (shards, filt_rows, span))], axis=1)
    send = send.reshape(shards * (3 * own_rows + filt_rows), span)
    recv = lax.all_to_all(send, "ctx", split_axis=0, concat_axis=1, tiled=True)
    length = recv.shape[1]
    tab = dft_tables(length)
    width = tab["width"]

    spec = forward_dft(recv, tab)
    outer = spec.shape[1]
    fspec = spec[: 3 * own_rows].reshape(3, own_rows // group_count, group_count, outer, 2 * width)
    hspec = spec[3 * own_rows :].reshape(2, 1, group_count, outer, 2 * width)
    conv_pol = cmul(fspec[0], hspec[0], False, width)
    conv_ref = cmul(fspec[1], hspec[1], False, width)
    corr = cmul(fspec[2], hspec[0], True, width)
    cross = jnp.sum(cmul(fspec[2], fspec[0], True, width), axis=0)
    prods = jnp.concatenate(
        [
            jnp.stack([conv_pol, conv_ref, corr]).reshape(3 * own_rows, outer, 2 * width),
            cross,
        ],
        axis=0,
    )
    back = inverse_dft(prods, tab)
    returned = lax.all_to_all(back, "ctx", split_axis=1, concat_axis=0, tiled=True)
    returned = returned.reshape(shards, 3 * own_rows + group_count, span)
    grad_filter = jnp.sum(returned[:, 3 * own_rows :], axis=0)
    grad_filter = lax.psum(grad_filter, "chan")
    returned = returned[:, : 3 * own_rows].reshape(shards, 3, own_rows, span)
    returned = returned.transpose(1, 0, 2, 3).reshape(3, chan_rows, span)

    mix_pol = returned[0] + skip_pol[:, None] * gated_pol
    mix_ref = returned[1] + skip_ref[:, None] * gated_ref
    grad_mix = returned[2] + skip_pol[:, None] * grad_sum
    out_pol = (query_pol.astype(jnp.float32) * mix_pol).astype(jnp.bfloat16)
    out_ref = (query_ref.astype(jnp.float32) * mix_ref).astype(jnp.bfloat16)
    grad_query = (out_grad * mix_pol).astype(jnp.bfloat16)
    grad_keys = (grad_mix * value_pol.astype(jnp.float32)).astype(jnp.bfloat16)
    grad_value = (grad_mix * keys_pol.astype(jnp.float32)).astype(jnp.bfloat16)
    return (out_pol, out_ref, grad_query, grad_keys, grad_value, grad_filter)


def solution(mesh):
    in_specs = (
        P("chan", "ctx"),
        P("chan", "ctx"),
        P("chan", "ctx"),
        P(None, "ctx"),
        P("chan"),
        P("chan", "ctx"),
        P("chan", "ctx"),
        P("chan", "ctx"),
        P(None, "ctx"),
        P("chan"),
        P("chan", "ctx"),
    )
    out_specs = (
        P("chan", "ctx"),
        P("chan", "ctx"),
        P("chan", "ctx"),
        P("chan", "ctx"),
        P("chan", "ctx"),
        P(None, "ctx"),
    )
    return jax.shard_map(local, mesh=mesh, in_specs=in_specs, out_specs=out_specs, check_vma=False)
```

profile of v0, /device:TPU:6, one launch (start us, length us, event | category | flops | bytes accessed | tf_op | source)
XLA Modules:
  0.0 249.0 jit_solution(8619886551938206708)
XLA Ops:
  0.6 0.7 pad_maximum_fusion.3
  1.3 1.1 convert_multiply_fusion.1
  2.4 1.1 convert_multiply_fusion.3
  3.5 1.1 convert_multiply_fusion.6
  4.9 108.4 %all_to_all.26 = f32[64,56,128]{2,1,0:T(8,128)S(1)} all-to-all(f32[64,56,128]{2,1,0:T(8,128)S(1)} %pad_maximum_fusion.1), channel_id=1, replica_groups=mesh['ctx'=64,'chan'=8] {'ctx'}, dimensions={0} | all-to-all | bytes 3670016 | tf_op jit(solution)/shard_map/all_to_all | solution.py:97
  113.2 3.1 %convolution_bitcast_fusion = f32[56,2,128,128]{2,3,1,0:T(8,128)S(1)} fusion(f32[2,128,64,1]{1,2,0,3:T(8,128)S(1)} %copy-done.12, f32[64,56,128]{2,1,0:T(8,128)S(1)} %all_to_all.26), kind=kOutput, calls=%fused_computation.19 | convolution fusion | flops 704643072 | bytes 9240576 | tf_op jit(solution)/shard_map/rab,cka->rckb/dot_general | solution.py:40
  116.4 1.7 multiply_add_fusion
  118.1 6.2 %fusion = f32[56,128,256]{2,1,0:T(8,128)S(1)} fusion(f32[256,256,1]{1,0,2:T(8,128)S(1)} %copy-done.6, f32[56,128,128]{1,2,0:T(8,128)S(1)} %get-tuple-element.7, f32[56,128,128]{1,2,0:T(8,128)S(1)} %get-tuple-element.6), kind=kOutput, calls=%fused_computation | convolution fusion | flops 2820407296 | bytes 14942208 | tf_op jit(solution)/shard_map/rkb,bm->rkm/dot_general | solution.py:46
  124.3 0.7 fusion.26
  125.2 0.3 multiply_subtract_fusion.3
  125.5 0.2 maximum_bitcast_fusion.1
  125.6 0.9 multiply_subtract_fusion.4
  126.6 0.2 maximum_bitcast_fusion
  126.8 0.2 maximum_bitcast_fusion.2
  127.0 0.6 pad_maximum_fusion
  127.6 0.3 copy-done.7
  127.9 3.0 %fusion.4 = f32[52,128,256]{2,1,0:T(8,128)S(1)} fusion(f32[256,256,1]{1,0,2:T(8,128)S(1)} %copy-done.7, f32[4,128,256]{2,1,0:T(8,128)S(1)} %maximum_reduce_fusion, f32[48,128,256]{2,1,0:T(8,128)S(1)} %bitcast.97), kind=kOutput, calls=%fused_computation.4 | convolution fusion | flops 2618949632 | bytes 13893632 | tf_op jit(solution)/shard_map/rkb,bm->rkm/dot_general | solution.py:52
  131.0 1.0 subtract_bitcast_fusion
  132.1 2.2 fusion.14
  134.2 1.0 copy.43
  135.2 94.9 %all_to_all.27 = f32[52,64,128]{2,0,1:T(8,128)S(1)} all-to-all(f32[52,64,128]{2,0,1:T(8,128)S(1)} %copy.43), channel_id=1, replica_groups=mesh['ctx'=64,'chan'=8] {'ctx'}, dimensions={1} | all-to-all | bytes 3407872 | tf_op jit(solution)/shard_map/all_to_all | solution.py:118
  230.4 16.1 %psum.7 = f32[4,128]{1,0:T(4,128)} all-reduce(f32[4,128]{1,0:T(4,128)S(1)} %slice_reduce_fusion), channel_id=1, replica_groups=mesh['ctx'=64,'chan'=8] {'chan'}, use_global_device_ids=true, to_apply=%region_2.0 | all-reduce | flops 512 | bytes 4096 | tf_op jit(solution)/shard_map/psum | solution.py:121
  246.7 1.4 fusion.20
  248.1 0.9 fusion.22
  (42 shorter events, 0.9 us)
Async XLA Ops:
  4.7 108.5 %copy-start.12 = (f32[2,128,64,1]{1,2,0,3:T(8,128)S(1)}, f32[2,128,64,1]{1,2,0,3:T(8,128)}, u32[]{:S(2)}) copy-start(f32[2,128,64,1]{1,2,0,3:T(8,128)} %constant.20) | copy-start | bytes 196612
  113.2 3.1 %copy-start.13 = (f32[128,128]{0,1:T(8,128)S(1)}, f32[128,128]{0,1:T(8,128)}, u32[]{:S(2)}) copy-start(f32[128,128]{0,1:T(8,128)} %constant.19.clone) | copy-start | bytes 196612
  113.2 3.1 %copy-start.14 = (f32[128,128]{0,1:T(8,128)S(1)}, f32[128,128]{0,1:T(8,128)}, u32[]{:S(2)}) copy-start(f32[128,128]{0,1:T(8,128)} %constant.18.clone) | copy-start | bytes 196612
  116.4 1.7 copy-start.6
  127.0 1.0 copy-start.7
  127.9 3.0 %copy-start.10 = (f32[128,128]{1,0:T(8,128)S(1)}, f32[128,128]{1,0:T(8,128)}, u32[]{:S(2)}) copy-start(f32[128,128]{1,0:T(8,128)} %constant.24) | copy-start | bytes 196612
  127.9 3.0 %copy-start.11 = (f32[128,128]{1,0:T(8,128)S(1)}, f32[128,128]{1,0:T(8,128)}, u32[]{:S(2)}) copy-start(f32[128,128]{1,0:T(8,128)} %constant.23) | copy-start | bytes 196612
  131.0 1.1 copy-start.9
  230.1 16.5 %copy-start = (bf16[1024,128]{1,0:T(8,128)(2,1)S(1)}, bf16[1024,128]{1,0:T(8,128)(2,1)}, u32[]{:S(2)}) copy-start(bf16[1024,128]{1,0:T(8,128)(2,1)} %param.27) | copy-start | bytes 786436
  230.1 16.5 %copy-start.1 = (bf16[1024,128]{1,0:T(8,128)(2,1)S(1)}, bf16[1024,128]{1,0:T(8,128)(2,1)}, u32[]{:S(2)}) copy-start(bf16[1024,128]{1,0:T(8,128)(2,1)} %param.17) | copy-start | bytes 786436
  230.1 16.5 %copy-start.2 = (bf16[1024,128]{1,0:T(8,128)(2,1)S(1)}, bf16[1024,128]{1,0:T(8,128)(2,1)}, u32[]{:S(2)}) copy-start(bf16[1024,128]{1,0:T(8,128)(2,1)} %param.19) | copy-start | bytes 786436
  230.1 16.5 %copy-start.3 = (bf16[1024,128]{1,0:T(8,128)(2,1)S(1)}, bf16[1024,128]{1,0:T(8,128)(2,1)}, u32[]{:S(2)}) copy-start(bf16[1024,128]{1,0:T(8,128)(2,1)} %param.18) | copy-start | bytes 786436
  230.1 16.5 %copy-start.15 = (f32[1024]{0:T(1024)S(1)}, f32[1024]{0:T(1024)}, u32[]{:S(2)}) copy-start(f32[1024]{0:T(1024)} %param.21) | copy-start | bytes 12292
  230.4 17.7 %copy-start.4 = (bf16[1024,128]{1,0:T(8,128)(2,1)S(1)}, bf16[1024,128]{1,0:T(8,128)(2,1)}, u32[]{:S(2)}) copy-start(bf16[1024,128]{1,0:T(8,128)(2,1)} %param.24) | copy-start | bytes 786436
  230.4 17.7 %copy-start.5 = (bf16[1024,128]{1,0:T(8,128)(2,1)S(1)}, bf16[1024,128]{1,0:T(8,128)(2,1)}, u32[]{:S(2)}) copy-start(bf16[1024,128]{1,0:T(8,128)(2,1)} %param.23) | copy-start | bytes 786436
  230.4 17.7 %copy-start.8 = (bf16[1024,128]{1,0:T(8,128)(2,1)S(1)}, bf16[1024,128]{1,0:T(8,128)(2,1)}, u32[]{:S(2)}) copy-start(bf16[1024,128]{1,0:T(8,128)(2,1)} %param.22) | copy-start | bytes 786436
  230.4 17.7 %copy-start.16 = (f32[1024]{0:T(1024)S(1)}, f32[1024]{0:T(1024)}, u32[]{:S(2)}) copy-start(f32[1024]{0:T(1024)} %param.26) | copy-start | bytes 12292
where the time goes:
time: 253 us; the launch traced here: 249 us
  blocking collectives  219 us (87%)
  matrix products  14.4 us (6%)
  other arithmetic  11.6 us (5%)
  local copies, waits for them, and re-layouts  2.54 us (1%)
    all_to_all x1, blocking collectives, local(): recv = lax.all_to_all(send, 'ctx', split_axis=0, concat_axis=1, tiled=True)  108 us
    all_to_all x1, blocking collectives, local(): lax.all_to_all(back, 'ctx', split_axis=1, concat_axis=0, tiled=True)  94.9 us
    psum x1, blocking collectives, local(): grad_filter = lax.psum(grad_filter, 'chan')  16.1 us
    dot_general x1, matrix products, forward_dft(): return jnp.einsum('rkb,bm->rkm', z, tab['fwd_b'], precision=PREC)  6.17 us

commit v1 on v0

--- a/solution.py
+++ b/solution.py
@@ -87,40 +87,51 @@
 
     shards = lax.axis_size("ctx")
     own_rows = chan_rows // shards
-    fields = jnp.stack([gated_pol, gated_ref, grad_sum])
-    fields = fields.reshape(3, shards, own_rows, span).transpose(1, 0, 2, 3)
-    fields = fields.reshape(shards, 3 * own_rows, span)
+
+    def to_channels(parts, extra):
+        count = len(parts)
+        block = jnp.stack(parts).reshape(count, shards, own_rows, span).transpose(1, 0, 2, 3)
+        block = block.reshape(shards, count * own_rows, span)
+        if extra is not None:
+            block = jnp.concatenate(
+                [block, jnp.broadcast_to(extra[None], (shards,) + extra.shape)], axis=1
+            )
+        block = block.reshape(-1, span)
+        return lax.all_to_all(block, "ctx", split_axis=0, concat_axis=1, tiled=True)
+
+    def to_positions(block, count):
+        got = lax.all_to_all(block, "ctx", split_axis=1, concat_axis=0, tiled=True)
+        got = got.reshape(shards, -1, span)
+        fields_back = got[:, : count * own_rows].reshape(shards, count, own_rows, span)
+        fields_back = fields_back.transpose(1, 0, 2, 3).reshape(count, chan_rows, span)
+        return fields_back, got[:, count * own_rows :]
+
     filt = jnp.concatenate([filter_pol, filter_ref], axis=0)
-    filt_rows = filt.shape[0]
-    send = jnp.concatenate([fields, jnp.broadcast_to(filt[None], (shards, filt_rows, span))], axis=1)
-    send = send.reshape(shards * (3 * own_rows + filt_rows), span)
-    recv = lax.all_to_all(send, "ctx", split_axis=0, concat_axis=1, tiled=True)
-    length = recv.shape[1]
+    recv_pol = to_channels([gated_pol, grad_sum], filt)
+    recv_ref = to_channels([gated_ref], None)
+    length = recv_pol.shape[1]
     tab = dft_tables(length)
     width = tab["width"]
+    groups_per = own_rows // group_count
 
-    spec = forward_dft(recv, tab)
+    spec = forward_dft(recv_pol, tab)
     outer = spec.shape[1]
-    fspec = spec[: 3 * own_rows].reshape(3, own_rows // group_count, group_count, outer, 2 * width)
-    hspec = spec[3 * own_rows :].reshape(2, 1, group_count, outer, 2 * width)
+    fspec = spec[: 2 * own_rows].reshape(2, groups_per, group_count, outer, 2 * width)
+    hspec = spec[2 * own_rows :].reshape(2, 1, group_count, outer, 2 * width)
     conv_pol = cmul(fspec[0], hspec[0], False, width)
-    conv_ref = cmul(fspec[1], hspec[1], False, width)
-    corr = cmul(fspec[2], hspec[0], True, width)
-    cross = jnp.sum(cmul(fspec[2], fspec[0], True, width), axis=0)
+    corr = cmul(fspec[1], hspec[0], True, width)
+    cross = jnp.sum(cmul(fspec[1], fspec[0], True, width), axis=0)
     prods = jnp.concatenate(
-        [
-            jnp.stack([conv_pol, conv_ref, corr]).reshape(3 * own_rows, outer, 2 * width),
-            cross,
-        ],
-        axis=0,
+        [jnp.stack([conv_pol, corr]).reshape(2 * own_rows, outer, 2 * width), cross], axis=0
     )
-    back = inverse_dft(prods, tab)
-    returned = lax.all_to_all(back, "ctx", split_axis=1, concat_axis=0, tiled=True)
-    returned = returned.reshape(shards, 3 * own_rows + group_count, span)
-    grad_filter = jnp.sum(returned[:, 3 * own_rows :], axis=0)
-    grad_filter = lax.psum(grad_filter, "chan")
-    returned = returned[:, : 3 * own_rows].reshape(shards, 3, own_rows, span)
-    returned = returned.transpose(1, 0, 2, 3).reshape(3, chan_rows, span)
+    pol_back, partial = to_positions(inverse_dft(prods, tab), 2)
+
+    spec_ref = forward_dft(recv_ref, tab).reshape(groups_per, group_count, outer, 2 * width)
+    conv_ref = cmul(spec_ref, hspec[1], False, width).reshape(own_rows, outer, 2 * width)
+    ref_back, _ = to_positions(inverse_dft(conv_ref, tab), 1)
+
+    grad_filter = lax.psum(jnp.sum(partial, axis=0), "chan")
+    returned = (pol_back[0], ref_back[0], pol_back[1])
 
     mix_pol = returned[0] + skip_pol[:, None] * gated_pol
     mix_ref = returned[1] + skip_ref[:, None] * gated_ref

time: 253 us -> 278 us (1.099)
  blocking collectives: 219 us -> 16 us
  waiting for transfers between devices: 0 us -> 183 us
  starting transfers between devices: 0 us -> 34.7 us
  local copies, waits for them, and re-layouts: 2.54 us -> 9.77 us
    all_to_all x2 -> x0, blocking collectives: 203 us -> none  [the longest x1 108 us: local(): recv = lax.all_to_all(send, 'ctx', split_axis=0, concat_axis=1, tiled=True)]
    all_to_all x0 -> x4, waiting for transfers between devices: none -> 183 us  [the longest x2 93.8 us: to_channels(): return lax.all_to_all(block, 'ctx', split_axis=0, concat_axis=1, tiled=True)]
    all_to_all x0 -> x4, starting transfers between devices: none -> 34.7 us  [the longest x2 24.2 us: to_channels(): return lax.all_to_all(block, 'ctx', split_axis=0, concat_axis=1, tiled=True)]
    unnamed x34 -> x42, local copies, waits for them, and re-layouts: 0.42 us -> 3.82 us
    dot_general x1 -> x2, matrix products: 6.17 us -> 6.35 us  [forward_dft(): return jnp.einsum('rkb,bm->rkm', z, tab['fwd_b'], precision=PREC)]
  transfers between devices with their start and end apart: 0 -> 4, of which waited for: 0 -> 4; matrix products, arithmetic and copies ran while one was open for 0% -> 6% of each run, Pallas kernels for 0% -> 0%
where the time goes in v1:
time: 278 us; the launch traced here: 273 us
  waiting for transfers between devices  183 us (66%)
  starting transfers between devices  34.7 us (12%)
  matrix products  16.4 us (6%)
  blocking collectives  16 us (6%)
  other arithmetic  11.9 us (4%)
  local copies, waits for them, and re-layouts  9.77 us (4%)
    all_to_all x2, waiting for transfers between devices, to_channels(): return lax.all_to_all(block, 'ctx', split_axis=0, concat_axis=1, tiled=True)  93.8 us
    all_to_all x2, waiting for transfers between devices, to_positions(): got = lax.all_to_all(block, 'ctx', split_axis=1, concat_axis=0, tiled=True)  89.5 us
    all_to_all x2, starting transfers between devices, to_channels(): return lax.all_to_all(block, 'ctx', split_axis=0, concat_axis=1, tiled=True)  24.2 us
    psum x1, blocking collectives, local(): grad_filter = lax.psum(jnp.sum(partial, axis=0), 'chan')  16 us
    all_to_all x2, starting transfers between devices, to_positions(): got = lax.all_to_all(block, 'ctx', split_axis=1, concat_axis=0, tiled=True)  10.5 us
    dot_general x2, matrix products, forward_dft(): return jnp.einsum('rkb,bm->rkm', z, tab['fwd_b'], precision=PREC)  6.35 us
  transfers between devices with their start and end apart: 4, of which 4 were waited for; matrix products, arithmetic and copies ran while one was open for 6% of the time, Pallas kernels for 0%

profile of v1, /device:TPU:6, one launch (start us, length us, event | category | flops | bytes accessed | tf_op | source)
XLA Modules:
  0.0 273.2 jit_solution(8185068048787870214)
XLA Ops:
  0.7 1.9 convert_multiply_fusion.6
  2.6 18.7 %all-to-all-start.2 = ((f32[64,16,128]{2,1,0:T(8,128)}), f32[64,16,128]{2,1,0:T(8,128)S(1)}, u32[]{:S(2)}, u32[]{:S(2)}) async-start(f32[64,16,128]{2,1,0:T(8,128)} %bitcast.33), calls=%async_computation.2 | async-start | bytes 1048576 | tf_op jit(solution)/shard_map/all_to_all | solution.py:100
  22.1 1.1 convert_multiply_fusion.3
  23.3 1.2 pad_maximum_fusion.2
  24.5 30.5 %all-to-all-done.2 = f32[64,16,128]{2,1,0:T(8,128)S(1)} async-done(((f32[64,16,128]{2,1,0:T(8,128)}), f32[64,16,128]{2,1,0:T(8,128)S(1)}, u32[]{:S(2)}, u32[]{:S(2)}) %all-to-all-start.2) | async-done | bytes 524320 | tf_op jit(solution)/shard_map/all_to_all | solution.py:100
  55.0 5.4 %all-to-all-start = ((f32[64,40,128]{2,1,0:T(8,128)}), f32[64,40,128]{2,1,0:T(8,128)S(1)}, u32[]{:S(2)}, u32[]{:S(2)}) async-start(f32[64,40,128]{2,1,0:T(8,128)} %pad_maximum_fusion.2), calls=%async_computation | async-start | bytes 2621440 | tf_op jit(solution)/shard_map/all_to_all | solution.py:100
  62.5 1.9 fusion.12
  64.4 63.3 %all-to-all-done = f32[64,40,128]{2,1,0:T(8,128)S(1)} async-done(((f32[64,40,128]{2,1,0:T(8,128)}), f32[64,40,128]{2,1,0:T(8,128)S(1)}, u32[]{:S(2)}, u32[]{:S(2)}) %all-to-all-start) | async-done | bytes 1310752 | tf_op jit(solution)/shard_map/all_to_all | solution.py:100
  127.6 3.1 %convolution_bitcast_fusion = f32[40,2,128,128]{2,3,1,0:T(8,128)S(1)} fusion(f32[2,128,64,1]{1,2,0,3:T(8,128)} %constant.20, f32[64,40,128]{2,1,0:T(8,128)S(1)} %all-to-all-done), kind=kOutput, calls=%fused_computation.17 | convolution fusion | flops 503316480 | bytes 6619136 | tf_op jit(solution)/shard_map/rab,cka->rckb/dot_general | solution.py:40
  130.8 1.1 multiply_add_fusion
  131.9 4.5 %fusion = f32[40,128,256]{2,1,0:T(8,128)S(1)} fusion(f32[256,256,1]{1,0,2:T(8,128)S(1)} %copy-done.11, f32[40,128,128]{1,2,0:T(8,128)S(1)} %get-tuple-element.7, f32[40,128,128]{1,2,0:T(8,128)S(1)} %get-tuple-element.6), kind=kOutput, calls=%fused_computation | convolution fusion | flops 2014576640 | bytes 10747904 | tf_op jit(solution)/shard_map/rkb,bm->rkm/dot_general | solution.py:46
  136.9 1.8 copy-done
  141.6 1.3 fusion.25
  142.9 1.1 copy.67
  144.0 5.3 %all-to-all-start.3 = ((f32[16,64,128]{2,0,1:T(8,128)}), f32[16,64,128]{2,0,1:T(8,128)S(1)}, u32[]{:S(2)}, u32[]{:S(2)}) async-start(f32[16,64,128]{2,0,1:T(8,128)} %copy.67), calls=%async_computation.3 | async-start | bytes 1048576 | tf_op jit(solution)/shard_map/all_to_all | solution.py:103
  149.2 2.7 fusion.41
  153.6 2.1 fusion.4
  156.4 1.5 fusion.20
  158.0 1.8 copy.60
  159.8 23.1 %all-to-all-done.3 = f32[16,64,128]{2,0,1:T(8,128)S(1)} async-done(((f32[16,64,128]{2,0,1:T(8,128)}), f32[16,64,128]{2,0,1:T(8,128)S(1)}, u32[]{:S(2)}, u32[]{:S(2)}) %all-to-all-start.3) | async-done | bytes 524320 | tf_op jit(solution)/shard_map/all_to_all | solution.py:103
  182.9 5.3 %all-to-all-start.1 = ((f32[36,64,128]{2,0,1:T(8,128)}), f32[36,64,128]{2,0,1:T(8,128)S(1)}, u32[]{:S(2)}, u32[]{:S(2)}) async-start(f32[36,64,128]{2,0,1:T(8,128)} %copy.60), calls=%async_computation.1 | async-start | bytes 2621440 | tf_op jit(solution)/shard_map/all_to_all | solution.py:103
  189.2 66.4 %all-to-all-done.1 = f32[36,64,128]{2,0,1:T(8,128)S(1)} async-done(((f32[36,64,128]{2,0,1:T(8,128)}), f32[36,64,128]{2,0,1:T(8,128)S(1)}, u32[]{:S(2)}, u32[]{:S(2)}) %all-to-all-start.1) | async-done | bytes 1179680 | tf_op jit(solution)/shard_map/all_to_all | solution.py:103
  255.9 16.0 %psum.7 = f32[4,128]{1,0:T(4,128)} all-reduce(f32[4,128]{1,0:T(4,128)S(1)} %slice_reduce_fusion), channel_id=1, replica_groups=mesh['ctx'=64,'chan'=8] {'chan'}, use_global_device_ids=true, to_apply=%region_2.0 | all-reduce | flops 512 | bytes 4096 | tf_op jit(solution)/shard_map/psum | solution.py:133
  271.9 1.4 fusion.31
  (63 shorter events, 9.7 us)
Async XLA Ops:
  0.6 22.5 %copy-start.4 = (bf16[1024,128]{1,0:T(8,128)(2,1)S(1)}, bf16[1024,128]{1,0:T(8,128)(2,1)}, u32[]{:S(2)}) copy-start(bf16[1024,128]{1,0:T(8,128)(2,1)} %param.17) | copy-start | bytes 786436
  0.6 22.5 %copy-start.2 = (bf16[1024,128]{1,0:T(8,128)(2,1)S(1)}, bf16[1024,128]{1,0:T(8,128)(2,1)}, u32[]{:S(2)}) copy-start(bf16[1024,128]{1,0:T(8,128)(2,1)} %param.27) | copy-start | bytes 786436
  2.6 52.4 %all-to-all-start.2 = ((f32[64,16,128]{2,1,0:T(8,128)}), f32[64,16,128]{2,1,0:T(8,128)S(1)}, u32[]{:S(2)}, u32[]{:S(2)}) async-start(f32[64,16,128]{2,1,0:T(8,128)} %bitcast.33), calls=%async_computation.2 | async-start | bytes 1048576 | tf_op jit(solution)/shard_map/all_to_all | solution.py:100
  23.3 37.1 %copy-start.15 = (f32[2,128,64,1]{1,2,0,3:T(8,128)S(1)}, f32[2,128,64,1]{1,2,0,3:T(8,128)}, u32[]{:S(2)}) copy-start(f32[2,128,64,1]{1,2,0,3:T(8,128)} %constant.20) | copy-start | bytes 196612
  24.5 37.0 %copy-start.12 = (f32[128,128]{0,1:T(8,128)S(1)}, f32[128,128]{0,1:T(8,128)}, u32[]{:S(2)}) copy-start(f32[128,128]{0,1:T(8,128)} %constant.18.clone) | copy-start | bytes 196612
  24.5 37.0 %copy-start.13 = (f32[128,128]{0,1:T(8,128)S(1)}, f32[128,128]{0,1:T(8,128)}, u32[]{:S(2)}) copy-start(f32[128,128]{0,1:T(8,128)} %constant.19.clone) | copy-start | bytes 196612
  55.0 72.6 %all-to-all-start = ((f32[64,40,128]{2,1,0:T(8,128)}), f32[64,40,128]{2,1,0:T(8,128)S(1)}, u32[]{:S(2)}, u32[]{:S(2)}) async-start(f32[64,40,128]{2,1,0:T(8,128)} %pad_maximum_fusion.2), calls=%async_computation | async-start | bytes 2621440 | tf_op jit(solution)/shard_map/all_to_all | solution.py:100
  61.5 1.0 copy-start.10
  130.8 1.1 copy-start.11
  136.4 2.3 copy-start
  138.7 0.9 copy-start.1
  144.0 38.9 %all-to-all-start.3 = ((f32[16,64,128]{2,0,1:T(8,128)}), f32[16,64,128]{2,0,1:T(8,128)S(1)}, u32[]{:S(2)}, u32[]{:S(2)}) async-start(f32[16,64,128]{2,0,1:T(8,128)} %copy.67), calls=%async_computation.3 | async-start | bytes 1048576 | tf_op jit(solution)/shard_map/all_to_all | solution.py:103
  153.6 2.1 copy-start.17
  153.6 2.1 copy-start.18
  158.0 30.2 %copy-start.8 = (bf16[1024,128]{1,0:T(8,128)(2,1)S(1)}, bf16[1024,128]{1,0:T(8,128)(2,1)}, u32[]{:S(2)}) copy-start(bf16[1024,128]{1,0:T(8,128)(2,1)} %param.24) | copy-start | bytes 786436
  158.0 30.2 %copy-start.9 = (bf16[1024,128]{1,0:T(8,128)(2,1)S(1)}, bf16[1024,128]{1,0:T(8,128)(2,1)}, u32[]{:S(2)}) copy-start(bf16[1024,128]{1,0:T(8,128)(2,1)} %param.23) | copy-start | bytes 786436
  158.0 30.2 %copy-start.16 = (bf16[1024,128]{1,0:T(8,128)(2,1)S(1)}, bf16[1024,128]{1,0:T(8,128)(2,1)}, u32[]{:S(2)}) copy-start(bf16[1024,128]{1,0:T(8,128)(2,1)} %param.22) | copy-start | bytes 786436
  158.0 30.2 %copy-start.19 = (f32[1024]{0:T(1024)S(1)}, f32[1024]{0:T(1024)}, u32[]{:S(2)}) copy-start(f32[1024]{0:T(1024)} %param.26) | copy-start | bytes 12292
  182.9 72.6 %all-to-all-start.1 = ((f32[36,64,128]{2,0,1:T(8,128)}), f32[36,64,128]{2,0,1:T(8,128)S(1)}, u32[]{:S(2)}, u32[]{:S(2)}) async-start(f32[36,64,128]{2,0,1:T(8,128)} %copy.60), calls=%async_computation.1 | async-start | bytes 2621440 | tf_op jit(solution)/shard_map/all_to_all | solution.py:103
  189.1 82.7 %copy-start.3 = (bf16[1024,128]{1,0:T(8,128)(2,1)S(1)}, bf16[1024,128]{1,0:T(8,128)(2,1)}, u32[]{:S(2)}) copy-start(bf16[1024,128]{1,0:T(8,128)(2,1)} %param.27) | copy-start | bytes 786436
  189.1 82.7 %copy-start.5 = (bf16[1024,128]{1,0:T(8,128)(2,1)S(1)}, bf16[1024,128]{1,0:T(8,128)(2,1)}, u32[]{:S(2)}) copy-start(bf16[1024,128]{1,0:T(8,128)(2,1)} %param.17) | copy-start | bytes 786436
  189.1 82.7 %copy-start.6 = (bf16[1024,128]{1,0:T(8,128)(2,1)S(1)}, bf16[1024,128]{1,0:T(8,128)(2,1)}, u32[]{:S(2)}) copy-start(bf16[1024,128]{1,0:T(8,128)(2,1)} %param.19) | copy-start | bytes 786436
  189.1 82.7 %copy-start.7 = (bf16[1024,128]{1,0:T(8,128)(2,1)S(1)}, bf16[1024,128]{1,0:T(8,128)(2,1)}, u32[]{:S(2)}) copy-start(bf16[1024,128]{1,0:T(8,128)(2,1)} %param.18) | copy-start | bytes 786436
  189.1 82.7 %copy-start.20 = (f32[1024]{0:T(1024)S(1)}, f32[1024]{0:T(1024)}, u32[]{:S(2)}) copy-start(f32[1024]{0:T(1024)} %param.21) | copy-start | bytes 12292
  (1 other events, 0.8 us)

commit v2 on v0

--- a/solution.py
+++ b/solution.py
@@ -87,12 +87,14 @@
 
     shards = lax.axis_size("ctx")
     own_rows = chan_rows // shards
+    blocks = shards // group_count
     fields = jnp.stack([gated_pol, gated_ref, grad_sum])
-    fields = fields.reshape(3, shards, own_rows, span).transpose(1, 0, 2, 3)
+    fields = fields.reshape(3, blocks, own_rows, group_count, span).transpose(1, 3, 0, 2, 4)
     fields = fields.reshape(shards, 3 * own_rows, span)
-    filt = jnp.concatenate([filter_pol, filter_ref], axis=0)
-    filt_rows = filt.shape[0]
-    send = jnp.concatenate([fields, jnp.broadcast_to(filt[None], (shards, filt_rows, span))], axis=1)
+    filt = jnp.stack([filter_pol, filter_ref], axis=1)
+    filt_rows = filt.shape[1]
+    filt = jnp.broadcast_to(filt[None], (blocks, group_count, filt_rows, span))
+    send = jnp.concatenate([fields, filt.reshape(shards, filt_rows, span)], axis=1)
     send = send.reshape(shards * (3 * own_rows + filt_rows), span)
     recv = lax.all_to_all(send, "ctx", split_axis=0, concat_axis=1, tiled=True)
     length = recv.shape[1]
@@ -101,26 +103,21 @@
 
     spec = forward_dft(recv, tab)
     outer = spec.shape[1]
-    fspec = spec[: 3 * own_rows].reshape(3, own_rows // group_count, group_count, outer, 2 * width)
-    hspec = spec[3 * own_rows :].reshape(2, 1, group_count, outer, 2 * width)
-    conv_pol = cmul(fspec[0], hspec[0], False, width)
-    conv_ref = cmul(fspec[1], hspec[1], False, width)
-    corr = cmul(fspec[2], hspec[0], True, width)
-    cross = jnp.sum(cmul(fspec[2], fspec[0], True, width), axis=0)
-    prods = jnp.concatenate(
-        [
-            jnp.stack([conv_pol, conv_ref, corr]).reshape(3 * own_rows, outer, 2 * width),
-            cross,
-        ],
-        axis=0,
-    )
+    fspec = spec[: 3 * own_rows].reshape(3, own_rows, outer, 2 * width)
+    hpol = spec[3 * own_rows : 3 * own_rows + 1]
+    href = spec[3 * own_rows + 1 :]
+    conv_pol = cmul(fspec[0], hpol, False, width)
+    conv_ref = cmul(fspec[1], href, False, width)
+    corr = cmul(fspec[2], hpol, True, width)
+    cross = jnp.sum(cmul(fspec[2], fspec[0], True, width), axis=0, keepdims=True)
+    prods = jnp.concatenate([conv_pol, conv_ref, corr, cross], axis=0)
     back = inverse_dft(prods, tab)
     returned = lax.all_to_all(back, "ctx", split_axis=1, concat_axis=0, tiled=True)
-    returned = returned.reshape(shards, 3 * own_rows + group_count, span)
-    grad_filter = jnp.sum(returned[:, 3 * own_rows :], axis=0)
+    returned = returned.reshape(blocks, group_count, 3 * own_rows + 1, span)
+    grad_filter = jnp.sum(returned[:, :, 3 * own_rows], axis=0)
     grad_filter = lax.psum(grad_filter, "chan")
-    returned = returned[:, : 3 * own_rows].reshape(shards, 3, own_rows, span)
-    returned = returned.transpose(1, 0, 2, 3).reshape(3, chan_rows, span)
+    returned = returned[:, :, : 3 * own_rows].reshape(blocks, group_count, 3, own_rows, span)
+    returned = returned.transpose(2, 0, 3, 1, 4).reshape(3, chan_rows, span)
 
     mix_pol = returned[0] + skip_pol[:, None] * gated_pol
     mix_ref = returned[1] + skip_ref[:, None] * gated_ref

time: 253 us -> 249 us (0.984)
  other arithmetic: 11.6 us -> 8.38 us
where the time goes in v2:
time: 249 us; the launch traced here: 245 us
  blocking collectives  219 us (88%)
  matrix products  13.8 us (6%)
  other arithmetic  8.38 us (3%)
  local copies, waits for them, and re-layouts  2.65 us (1%)
    all_to_all x1, blocking collectives, local(): recv = lax.all_to_all(send, 'ctx', split_axis=0, concat_axis=1, tiled=True)  108 us
    all_to_all x1, blocking collectives, local(): lax.all_to_all(back, 'ctx', split_axis=1, concat_axis=0, tiled=True)  94.9 us
    psum x1, blocking collectives, local(): grad_filter = lax.psum(grad_filter, 'chan')  16.1 us
    dot_general x1, matrix products, forward_dft(): return jnp.einsum('rkb,bm->rkm', z, tab['fwd_b'], precision=PREC)  5.66 us

profile of v2, /device:TPU:6, one launch (start us, length us, event | category | flops | bytes accessed | tf_op | source)
XLA Modules:
  0.0 245.3 jit_solution(10863066289735112354)
XLA Ops:
  0.7 1.1 convert_multiply_fusion.3
  1.9 1.1 convert_multiply_fusion.6
  3.0 0.1 convert_multiply_fusion.1
  3.2 0.1 pad_maximum_fusion.1
  3.3 0.1 pad_maximum_fusion
  3.4 108.4 %all_to_all.26 = f32[64,50,128]{2,1,0:T(8,128)S(1)} all-to-all(f32[64,50,128]{2,1,0:T(8,128)S(1)} %pad_maximum_fusion), channel_id=1, replica_groups=mesh['ctx'=64,'chan'=8] {'ctx'}, dimensions={0} | all-to-all | bytes 3276800 | tf_op jit(solution)/shard_map/all_to_all | solution.py:99
  111.8 2.8 %convolution_bitcast_fusion = f32[50,2,128,128]{2,3,1,0:T(8,128)S(1)} fusion(f32[2,128,64,1]{1,2,0,3:T(8,128)S(1)} %copy-done.11, f32[64,50,128]{2,1,0:T(8,128)S(1)} %all_to_all.26), kind=kOutput, calls=%fused_computation.28 | convolution fusion | flops 629145600 | bytes 8257536 | tf_op jit(solution)/shard_map/rab,cka->rckb/dot_general | solution.py:40
  114.7 1.5 multiply_add_fusion
  116.1 5.7 %fusion = f32[50,128,256]{2,1,0:T(8,128)S(1)} fusion(f32[256,256,1]{1,0,2:T(8,128)S(1)} %copy-done.6, f32[50,128,128]{1,2,0:T(8,128)S(1)} %get-tuple-element.13, f32[50,128,128]{1,2,0:T(8,128)S(1)} %get-tuple-element.12), kind=kOutput, calls=%fused_computation | convolution fusion | flops 2518220800 | bytes 13369344 | tf_op jit(solution)/shard_map/rkb,bm->rkm/dot_general | solution.py:46
  121.8 0.7 multiply_subtract_fusion.4
  122.6 0.1 maximum_reduce_fusion
  122.7 0.3 multiply_subtract_fusion.3
  123.0 0.5 copy-done.18
  123.5 3.4 %fusion.4 = f32[49,128,256]{2,1,0:T(8,128)S(1)} fusion(f32[256,256,1]{1,0,2:T(8,128)S(1)} %copy-done.18, f32[1,128,256]{2,1,0:T(8,128)S(1)} %bitcast.81, f32[16,128,128]{2,1,0:T(8,128)S(1)} %get-tuple-element.8, f32[16,128,128]{2,1,0:T(8,128)S(1)} %get-tuple-element.7, f32[16,128,128]{2,1,0:T(8,128)S(1)} %get-tuple-element.11, ...), kind=kOutput, calls=%fused_computation.4 | convolution fusion | flops 2475884544 | bytes 13107200 | tf_op jit(solution)/shard_map/rkb,bm->rkm/dot_general | solution.py:52
  127.0 1.0 subtract_bitcast_fusion
  128.0 1.9 fusion.24
  129.9 0.9 copy.42
  130.8 94.9 %all_to_all.27 = f32[49,64,128]{2,0,1:T(8,128)S(1)} all-to-all(f32[49,64,128]{2,0,1:T(8,128)S(1)} %copy.42), channel_id=1, replica_groups=mesh['ctx'=64,'chan'=8] {'ctx'}, dimensions={1} | all-to-all | bytes 3211264 | tf_op jit(solution)/shard_map/all_to_all | solution.py:115
  225.7 0.1 slice.123
  225.9 0.7 copy.54
  226.7 0.2 fusion.34
  226.8 16.1 %psum.7 = f32[4,128]{1,0:T(4,128)} all-reduce(f32[4,128]{1,0:T(4,128)S(1)} %slice_reduce_fusion), channel_id=1, replica_groups=mesh['ctx'=64,'chan'=8] {'chan'}, use_global_device_ids=true, to_apply=%region_2.0 | all-reduce | flops 512 | bytes 4096 | tf_op jit(solution)/shard_map/psum | solution.py:118
  243.0 1.4 fusion.30
  244.3 0.9 multiply_convert_fusion
  (45 shorter events, 0.3 us)
Async XLA Ops:
  0.6 2.4 copy-start.1
  0.6 2.4 copy-start
  0.7 2.5 %copy-start.17 = (f32[4,128]{1,0:T(4,128)S(1)}, f32[4,128]{1,0:T(4,128)}, u32[]{:S(2)}) copy-start(f32[4,128]{1,0:T(4,128)} %param.20) | copy-start | bytes 6148
  0.7 2.5 %copy-start.16 = (f32[4,128]{1,0:T(4,128)S(1)}, f32[4,128]{1,0:T(4,128)}, u32[]{:S(2)}) copy-start(f32[4,128]{1,0:T(4,128)} %param.25) | copy-start | bytes 6148
  3.3 108.5 %copy-start.11 = (f32[2,128,64,1]{1,2,0,3:T(8,128)S(1)}, f32[2,128,64,1]{1,2,0,3:T(8,128)}, u32[]{:S(2)}) copy-start(f32[2,128,64,1]{1,2,0,3:T(8,128)} %constant.20) | copy-start | bytes 196612
  111.8 2.8 %copy-start.12 = (f32[128,128]{0,1:T(8,128)S(1)}, f32[128,128]{0,1:T(8,128)}, u32[]{:S(2)}) copy-start(f32[128,128]{0,1:T(8,128)} %constant.18.clone) | copy-start | bytes 196612
  111.8 2.8 %copy-start.13 = (f32[128,128]{0,1:T(8,128)S(1)}, f32[128,128]{0,1:T(8,128)}, u32[]{:S(2)}) copy-start(f32[128,128]{0,1:T(8,128)} %constant.19.clone) | copy-start | bytes 196612
  114.6 1.5 copy-start.6
  122.5 1.0 copy-start.18
  123.5 3.5 %copy-start.9 = (f32[128,128]{1,0:T(8,128)S(1)}, f32[128,128]{1,0:T(8,128)}, u32[]{:S(2)}) copy-start(f32[128,128]{1,0:T(8,128)} %constant.23) | copy-start | bytes 196612
  123.5 3.5 %copy-start.10 = (f32[128,128]{1,0:T(8,128)S(1)}, f32[128,128]{1,0:T(8,128)}, u32[]{:S(2)}) copy-start(f32[128,128]{1,0:T(8,128)} %constant.24) | copy-start | bytes 196612
  127.0 1.0 copy-start.8
  225.8 17.1 %copy-start.2 = (bf16[1024,128]{1,0:T(8,128)(2,1)S(1)}, bf16[1024,128]{1,0:T(8,128)(2,1)}, u32[]{:S(2)}) copy-start(bf16[1024,128]{1,0:T(8,128)(2,1)} %param.19) | copy-start | bytes 786436
  225.9 17.1 %copy-start.3 = (bf16[1024,128]{1,0:T(8,128)(2,1)S(1)}, bf16[1024,128]{1,0:T(8,128)(2,1)}, u32[]{:S(2)}) copy-start(bf16[1024,128]{1,0:T(8,128)(2,1)} %param.18) | copy-start | bytes 786436
  225.9 17.1 %copy-start.14 = (f32[1024]{0:T(1024)S(1)}, f32[1024]{0:T(1024)}, u32[]{:S(2)}) copy-start(f32[1024]{0:T(1024)} %param.21) | copy-start | bytes 12292
  226.6 17.7 %copy-start.4 = (bf16[1024,128]{1,0:T(8,128)(2,1)S(1)}, bf16[1024,128]{1,0:T(8,128)(2,1)}, u32[]{:S(2)}) copy-start(bf16[1024,128]{1,0:T(8,128)(2,1)} %param.24) | copy-start | bytes 786436
  226.6 17.7 %copy-start.5 = (bf16[1024,128]{1,0:T(8,128)(2,1)S(1)}, bf16[1024,128]{1,0:T(8,128)(2,1)}, u32[]{:S(2)}) copy-start(bf16[1024,128]{1,0:T(8,128)(2,1)} %param.23) | copy-start | bytes 786436
  226.6 17.7 %copy-start.7 = (bf16[1024,128]{1,0:T(8,128)(2,1)S(1)}, bf16[1024,128]{1,0:T(8,128)(2,1)}, u32[]{:S(2)}) copy-start(bf16[1024,128]{1,0:T(8,128)(2,1)} %param.22) | copy-start | bytes 786436
  226.7 17.7 %copy-start.15 = (f32[1024]{0:T(1024)S(1)}, f32[1024]{0:T(1024)}, u32[]{:S(2)}) copy-start(f32[1024]{0:T(1024)} %param.26) | copy-start | bytes 12292

commit v3 on v2

--- a/solution.py
+++ b/solution.py
@@ -115,7 +115,12 @@
     returned = lax.all_to_all(back, "ctx", split_axis=1, concat_axis=0, tiled=True)
     returned = returned.reshape(blocks, group_count, 3 * own_rows + 1, span)
     grad_filter = jnp.sum(returned[:, :, 3 * own_rows], axis=0)
-    grad_filter = lax.psum(grad_filter, "chan")
+    chan_size = lax.axis_size("chan")
+    bit = 1
+    while bit < chan_size:
+        pairs = [(i, i ^ bit) for i in range(chan_size)]
+        grad_filter = grad_filter + lax.ppermute(grad_filter, "chan", pairs)
+        bit *= 2
     returned = returned[:, :, : 3 * own_rows].reshape(blocks, group_count, 3, own_rows, span)
     returned = returned.transpose(2, 0, 3, 1, 4).reshape(3, chan_rows, span)
 

time: 249 us -> 245 us (0.984); the launches traced: 245 us -> 245 us
  blocking collectives: 219 us -> 203 us
  starting transfers between devices: 0 us -> 8.74 us
  waiting for transfers between devices: 0 us -> 6.07 us
    psum x1 -> x0, blocking collectives: 16.1 us -> none  [local(): grad_filter = lax.psum(grad_filter, 'chan')]
    ppermute x0 -> x3, starting transfers between devices: none -> 8.74 us  [local(): grad_filter = grad_filter + lax.ppermute(grad_filter, 'chan', pairs)]
    ppermute x0 -> x3, waiting for transfers between devices: none -> 6.07 us  [local(): grad_filter = grad_filter + lax.ppermute(grad_filter, 'chan', pairs)]
  transfers between devices with their start and end apart: 0 -> 3, of which waited for: 0 -> 3; matrix products, arithmetic and copies ran while one was open for 0% -> 1% of each run, Pallas kernels for 0% -> 0%
where the time goes in v3:
time: 245 us
  blocking collectives  203 us (83%)
  matrix products  13.8 us (6%)
  other arithmetic  8.99 us (4%)
  starting transfers between devices  8.74 us (4%)
  waiting for transfers between devices  6.07 us (2%)
  local copies, waits for them, and re-layouts  2.59 us (1%)
    all_to_all x1, blocking collectives, local(): recv = lax.all_to_all(send, 'ctx', split_axis=0, concat_axis=1, tiled=True)  108 us
    all_to_all x1, blocking collectives, local(): lax.all_to_all(back, 'ctx', split_axis=1, concat_axis=0, tiled=True)  94.9 us
    ppermute x3, starting transfers between devices, local(): grad_filter = grad_filter + lax.ppermute(grad_filter, 'chan', pairs)  8.74 us
    ppermute x3, waiting for transfers between devices, local(): grad_filter = grad_filter + lax.ppermute(grad_filter, 'chan', pairs)  6.07 us
    dot_general x1, matrix products, forward_dft(): return jnp.einsum('rkb,bm->rkm', z, tab['fwd_b'], precision=PREC)  5.66 us
  transfers between devices with their start and end apart: 3, of which 3 were waited for; matrix products, arithmetic and copies ran while one was open for 1% of the time, Pallas kernels for 0%

profile of v3, /device:TPU:6, one launch (start us, length us, event | category | flops | bytes accessed | tf_op | source)
XLA Modules:
  0.0 244.6 jit_solution(11042577198170352278)
XLA Ops:
  0.7 1.1 convert_multiply_fusion.3
  1.9 1.1 convert_multiply_fusion.6
  3.4 108.4 %all_to_all.26 = f32[64,50,128]{2,1,0:T(8,128)S(1)} all-to-all(f32[64,50,128]{2,1,0:T(8,128)S(1)} %pad_maximum_fusion), channel_id=1, replica_groups=mesh['ctx'=64,'chan'=8] {'ctx'}, dimensions={0} | all-to-all | bytes 3276800 | tf_op jit(solution)/shard_map/all_to_all | solution.py:99
  111.8 2.8 %convolution_bitcast_fusion = f32[50,2,128,128]{2,3,1,0:T(8,128)S(1)} fusion(f32[2,128,64,1]{1,2,0,3:T(8,128)S(1)} %copy-done.11, f32[64,50,128]{2,1,0:T(8,128)S(1)} %all_to_all.26), kind=kOutput, calls=%fused_computation.28 | convolution fusion | flops 629145600 | bytes 8257536 | tf_op jit(solution)/shard_map/rab,cka->rckb/dot_general | solution.py:40
  114.7 1.5 multiply_add_fusion
  116.1 5.7 %fusion = f32[50,128,256]{2,1,0:T(8,128)S(1)} fusion(f32[256,256,1]{1,0,2:T(8,128)S(1)} %copy-done.6, f32[50,128,128]{1,2,0:T(8,128)S(1)} %get-tuple-element.13, f32[50,128,128]{1,2,0:T(8,128)S(1)} %get-tuple-element.12), kind=kOutput, calls=%fused_computation | convolution fusion | flops 2518220800 | bytes 13369344 | tf_op jit(solution)/shard_map/rkb,bm->rkm/dot_general | solution.py:46
  121.8 0.7 multiply_subtract_fusion.4
  122.7 0.3 multiply_subtract_fusion.3
  123.0 0.5 copy-done.18
  123.5 3.4 %fusion.4 = f32[49,128,256]{2,1,0:T(8,128)S(1)} fusion(f32[256,256,1]{1,0,2:T(8,128)S(1)} %copy-done.18, f32[1,128,256]{2,1,0:T(8,128)S(1)} %bitcast.81, f32[16,128,128]{2,1,0:T(8,128)S(1)} %get-tuple-element.8, f32[16,128,128]{2,1,0:T(8,128)S(1)} %get-tuple-element.7, f32[16,128,128]{2,1,0:T(8,128)S(1)} %get-tuple-element.11, ...), kind=kOutput, calls=%fused_computation.4 | convolution fusion | flops 2475884544 | bytes 13107200 | tf_op jit(solution)/shard_map/rkb,bm->rkm/dot_general | solution.py:52
  127.0 1.0 subtract_bitcast_fusion
  128.0 1.9 fusion.24
  129.9 0.9 copy.42
  130.8 94.9 %all_to_all.27 = f32[49,64,128]{2,0,1:T(8,128)S(1)} all-to-all(f32[49,64,128]{2,0,1:T(8,128)S(1)} %copy.42), channel_id=1, replica_groups=mesh['ctx'=64,'chan'=8] {'ctx'}, dimensions={1} | all-to-all | bytes 3211264 | tf_op jit(solution)/shard_map/all_to_all | solution.py:115
  225.9 2.7 %collective-permute-start = (f32[4,128]{1,0:T(4,128)S(1)}, f32[4,128]{1,0:T(4,128)S(1)}, u32[]{:S(2)}, u32[]{:S(2)}) collective-permute-start(f32[4,128]{1,0:T(4,128)S(1)} %slice_reduce_fusion), channel_id=1, source_target_pairs={{0,1},{1,0},{2,3},{3,2},{4,5},{5,4},{6,7},{7,6},{8,9},{9,8},{10,11... | collective-permute-start | bytes 6152 | tf_op jit(solution)/shard_map/ppermute | solution.py:122
  228.6 0.7 copy.54
  229.5 2.0 collective-permute-done
  231.5 2.7 %collective-permute-start.1 = (f32[4,128]{1,0:T(4,128)S(1)}, f32[4,128]{1,0:T(4,128)S(1)}, u32[]{:S(2)}, u32[]{:S(2)}) collective-permute-start(f32[4,128]{1,0:T(4,128)S(1)} %add.45), channel_id=1, source_target_pairs={{0,2},{1,3},{2,0},{3,1},{4,6},{5,7},{6,4},{7,5},{8,10},{9,11},{10,... | collective-permute-start | bytes 6152 | tf_op jit(solution)/shard_map/ppermute | solution.py:122
  234.3 1.4 fusion.30
  235.7 1.3 collective-permute-done.1
  237.0 3.3 %collective-permute-start.2 = (f32[4,128]{1,0:T(4,128)S(1)}, f32[4,128]{1,0:T(4,128)S(1)}, u32[]{:S(2)}, u32[]{:S(2)}) collective-permute-start(f32[4,128]{1,0:T(4,128)S(1)} %add.46), channel_id=1, source_target_pairs={{0,4},{1,5},{2,6},{3,7},{4,0},{5,1},{6,2},{7,3},{8,12},{9,13},{10,... | collective-permute-start | bytes 6152 | tf_op jit(solution)/shard_map/ppermute | solution.py:122
  240.4 0.9 multiply_convert_fusion
  241.3 2.7 %collective-permute-done.2 = f32[4,128]{1,0:T(4,128)S(1)} collective-permute-done((f32[4,128]{1,0:T(4,128)S(1)}, f32[4,128]{1,0:T(4,128)S(1)}, u32[]{:S(2)}, u32[]{:S(2)}) %collective-permute-start.2) | collective-permute-done | bytes 2080 | tf_op jit(solution)/shard_map/ppermute | solution.py:122
  244.0 0.6 add.47
  (53 shorter events, 0.9 us)
Async XLA Ops:
  0.6 2.4 copy-start.1
  0.6 2.4 copy-start
  0.7 2.5 %copy-start.17 = (f32[4,128]{1,0:T(4,128)S(1)}, f32[4,128]{1,0:T(4,128)}, u32[]{:S(2)}) copy-start(f32[4,128]{1,0:T(4,128)} %param.20) | copy-start | bytes 6148
  0.7 2.5 %copy-start.16 = (f32[4,128]{1,0:T(4,128)S(1)}, f32[4,128]{1,0:T(4,128)}, u32[]{:S(2)}) copy-start(f32[4,128]{1,0:T(4,128)} %param.25) | copy-start | bytes 6148
  3.3 108.5 %copy-start.11 = (f32[2,128,64,1]{1,2,0,3:T(8,128)S(1)}, f32[2,128,64,1]{1,2,0,3:T(8,128)}, u32[]{:S(2)}) copy-start(f32[2,128,64,1]{1,2,0,3:T(8,128)} %constant.20) | copy-start | bytes 196612
  111.8 2.8 %copy-start.12 = (f32[128,128]{0,1:T(8,128)S(1)}, f32[128,128]{0,1:T(8,128)}, u32[]{:S(2)}) copy-start(f32[128,128]{0,1:T(8,128)} %constant.18.clone) | copy-start | bytes 196612
  111.8 2.8 %copy-start.13 = (f32[128,128]{0,1:T(8,128)S(1)}, f32[128,128]{0,1:T(8,128)}, u32[]{:S(2)}) copy-start(f32[128,128]{0,1:T(8,128)} %constant.19.clone) | copy-start | bytes 196612
  114.6 1.5 copy-start.6
  122.5 1.0 copy-start.18
  123.5 3.5 %copy-start.9 = (f32[128,128]{1,0:T(8,128)S(1)}, f32[128,128]{1,0:T(8,128)}, u32[]{:S(2)}) copy-start(f32[128,128]{1,0:T(8,128)} %constant.23) | copy-start | bytes 196612
  123.5 3.5 %copy-start.10 = (f32[128,128]{1,0:T(8,128)S(1)}, f32[128,128]{1,0:T(8,128)}, u32[]{:S(2)}) copy-start(f32[128,128]{1,0:T(8,128)} %constant.24) | copy-start | bytes 196612
  127.0 1.0 copy-start.8
  225.9 8.4 %copy-start.2 = (bf16[1024,128]{1,0:T(8,128)(2,1)S(1)}, bf16[1024,128]{1,0:T(8,128)(2,1)}, u32[]{:S(2)}) copy-start(bf16[1024,128]{1,0:T(8,128)(2,1)} %param.19) | copy-start | bytes 786436
  225.9 8.4 %copy-start.3 = (bf16[1024,128]{1,0:T(8,128)(2,1)S(1)}, bf16[1024,128]{1,0:T(8,128)(2,1)}, u32[]{:S(2)}) copy-start(bf16[1024,128]{1,0:T(8,128)(2,1)} %param.18) | copy-start | bytes 786436
  225.9 8.4 %copy-start.14 = (f32[1024]{0:T(1024)S(1)}, f32[1024]{0:T(1024)}, u32[]{:S(2)}) copy-start(f32[1024]{0:T(1024)} %param.21) | copy-start | bytes 12292
  225.9 5.6 %collective-permute-start = (f32[4,128]{1,0:T(4,128)S(1)}, f32[4,128]{1,0:T(4,128)S(1)}, u32[]{:S(2)}, u32[]{:S(2)}) collective-permute-start(f32[4,128]{1,0:T(4,128)S(1)} %slice_reduce_fusion), channel_id=1, source_target_pairs={{0,1},{1,0},{2,3},{3,2},{4,5},{5,4},{6,7},{7,6},{8,9},{9,8},{10,11... | collective-permute-start | bytes 6152 | tf_op jit(solution)/shard_map/ppermute | solution.py:122
  229.3 11.0 %copy-start.4 = (bf16[1024,128]{1,0:T(8,128)(2,1)S(1)}, bf16[1024,128]{1,0:T(8,128)(2,1)}, u32[]{:S(2)}) copy-start(bf16[1024,128]{1,0:T(8,128)(2,1)} %param.24) | copy-start | bytes 786436
  229.4 11.0 %copy-start.5 = (bf16[1024,128]{1,0:T(8,128)(2,1)S(1)}, bf16[1024,128]{1,0:T(8,128)(2,1)}, u32[]{:S(2)}) copy-start(bf16[1024,128]{1,0:T(8,128)(2,1)} %param.23) | copy-start | bytes 786436
  229.4 11.0 %copy-start.7 = (bf16[1024,128]{1,0:T(8,128)(2,1)S(1)}, bf16[1024,128]{1,0:T(8,128)(2,1)}, u32[]{:S(2)}) copy-start(bf16[1024,128]{1,0:T(8,128)(2,1)} %param.22) | copy-start | bytes 786436
  229.4 11.0 %copy-start.15 = (f32[1024]{0:T(1024)S(1)}, f32[1024]{0:T(1024)}, u32[]{:S(2)}) copy-start(f32[1024]{0:T(1024)} %param.26) | copy-start | bytes 12292
  231.5 5.5 %collective-permute-start.1 = (f32[4,128]{1,0:T(4,128)S(1)}, f32[4,128]{1,0:T(4,128)S(1)}, u32[]{:S(2)}, u32[]{:S(2)}) collective-permute-start(f32[4,128]{1,0:T(4,128)S(1)} %add.45), channel_id=1, source_target_pairs={{0,2},{1,3},{2,0},{3,1},{4,6},{5,7},{6,4},{7,5},{8,10},{9,11},{10,... | collective-permute-start | bytes 6152 | tf_op jit(solution)/shard_map/ppermute | solution.py:122
  237.0 7.0 %collective-permute-start.2 = (f32[4,128]{1,0:T(4,128)S(1)}, f32[4,128]{1,0:T(4,128)S(1)}, u32[]{:S(2)}, u32[]{:S(2)}) collective-permute-start(f32[4,128]{1,0:T(4,128)S(1)} %add.46), channel_id=1, source_target_pairs={{0,4},{1,5},{2,6},{3,7},{4,0},{5,1},{6,2},{7,3},{8,12},{9,13},{10,... | collective-permute-start | bytes 6152 | tf_op jit(solution)/shard_map/ppermute | solution.py:122

commit v4 on v3

--- a/solution.py
+++ b/solution.py
@@ -8,6 +8,7 @@
 
 PREC = lax.Precision.HIGH
 LANES = 128
+NEAR = 4
 
 
 def dft_tables(length):
@@ -65,6 +66,19 @@
     return jnp.concatenate([xr * hr - xi * hi, xr * hi + xi * hr], axis=-1)
 
 
+def two_stage_all_to_all(block, near):
+    shards = block.shape[0]
+    far = shards // near
+    near_groups = [[f * near + r for r in range(near)] for f in range(far)]
+    far_groups = [[f * near + r for f in range(far)] for r in range(near)]
+    rest = block.shape[1:]
+    step = block.reshape((far, near) + rest).swapaxes(0, 1)
+    step = lax.all_to_all(step, "ctx", 0, 0, axis_index_groups=near_groups, tiled=True)
+    step = step.swapaxes(0, 1)
+    step = lax.all_to_all(step, "ctx", 0, 0, axis_index_groups=far_groups, tiled=True)
+    return step.reshape((shards,) + rest)
+
+
 def local(
     query_pol,
     keys_pol,
@@ -95,8 +109,8 @@
     filt_rows = filt.shape[1]
     filt = jnp.broadcast_to(filt[None], (blocks, group_count, filt_rows, span))
     send = jnp.concatenate([fields, filt.reshape(shards, filt_rows, span)], axis=1)
-    send = send.reshape(shards * (3 * own_rows + filt_rows), span)
-    recv = lax.all_to_all(send, "ctx", split_axis=0, concat_axis=1, tiled=True)
+    recv = two_stage_all_to_all(send, NEAR)
+    recv = recv.transpose(1, 0, 2).reshape(3 * own_rows + filt_rows, shards * span)
     length = recv.shape[1]
     tab = dft_tables(length)
     width = tab["width"]
@@ -112,7 +126,8 @@
     cross = jnp.sum(cmul(fspec[2], fspec[0], True, width), axis=0, keepdims=True)
     prods = jnp.concatenate([conv_pol, conv_ref, corr, cross], axis=0)
     back = inverse_dft(prods, tab)
-    returned = lax.all_to_all(back, "ctx", split_axis=1, concat_axis=0, tiled=True)
+    back = back.reshape(back.shape[0], shards, span).transpose(1, 0, 2)
+    returned = two_stage_all_to_all(back, NEAR)
     returned = returned.reshape(blocks, group_count, 3 * own_rows + 1, span)
     grad_filter = jnp.sum(returned[:, :, 3 * own_rows], axis=0)
     chan_size = lax.axis_size("chan")

time: 245 us -> 272 us (1.11)
  blocking collectives: 203 us -> 228 us
    all_to_all x2 -> x4, blocking collectives: 203 us -> 228 us  [the longest x2 177 us: two_stage_all_to_all(): lax.all_to_all(step, 'ctx', 0, 0, axis_index_groups=far_groups, tiled=True)]
where the time goes in v4:
time: 272 us
  blocking collectives  228 us (84%)
  matrix products  14.2 us (5%)
  other arithmetic  9.07 us (3%)
  starting transfers between devices  8.75 us (3%)
  waiting for transfers between devices  6.59 us (2%)
  local copies, waits for them, and re-layouts  4.05 us (1%)
    all_to_all x2, blocking collectives, two_stage_all_to_all(): lax.all_to_all(step, 'ctx', 0, 0, axis_index_groups=far_groups, tiled=True)  177 us
    all_to_all x2, blocking collectives, two_stage_all_to_all(): lax.all_to_all(step, 'ctx', 0, 0, axis_index_groups=near_groups, tiled=True)  50.8 us
    ppermute x3, starting transfers between devices, local(): grad_filter = grad_filter + lax.ppermute(grad_filter, 'chan', pairs)  8.75 us
    ppermute x3, waiting for transfers between devices, local(): grad_filter = grad_filter + lax.ppermute(grad_filter, 'chan', pairs)  6.59 us
    dot_general x1, matrix products, forward_dft(): return jnp.einsum('rkb,bm->rkm', z, tab['fwd_b'], precision=PREC)  5.66 us
  transfers between devices with their start and end apart: 3, of which 3 were waited for; matrix products, arithmetic and copies ran while one was open for 1% of the time, Pallas kernels for 0%

profile of v4, /device:TPU:6, one launch (start us, length us, event | category | flops | bytes accessed | tf_op | source)
XLA Modules:
  0.0 272.0 jit_solution(14317068448376591286)
XLA Ops:
  0.7 1.1 convert_multiply_fusion.3
  2.1 1.1 convert_multiply_fusion.6
  4.3 26.5 %all_to_all.20 = f32[4,16,50,128]{3,1,2,0:T(8,128)S(1)} all-to-all(f32[4,16,50,128]{3,1,2,0:T(8,128)S(1)} %maximum_bitcast_fusion), channel_id=1, replica_groups={{0,8,16,24},{32,40,48,56},{64,72,80,88},{96,104,112,120},{128,136,144,1..., dimensions={0} | all-to-all | bytes 3276800 | tf_op jit(solution)/shard_map/all_to_all | solution.py:76
  30.8 1.1 copy.34
  31.9 94.9 %all_to_all.21 = f32[16,4,50,128]{3,1,2,0:T(4,128)S(1)} all-to-all(f32[16,4,50,128]{3,1,2,0:T(4,128)S(1)} %copy.34), channel_id=1, replica_groups={{0,32,64,96,128,160,192,224,256,288,320,352,384,416,448,480},{8,40,72,1..., dimensions={0} | all-to-all | bytes 3276800 | tf_op jit(solution)/shard_map/all_to_all | solution.py:78
  127.3 2.8 %convolution_bitcast_fusion = f32[50,2,128,128]{2,3,1,0:T(8,128)S(1)} fusion(f32[50,64,128,1]{2,1,3,0:T(8,128)S(1)} %bitcast.75, f32[2,128,64,1]{1,2,0,3:T(8,128)S(1)} %copy-done.11), kind=kOutput, calls=%fused_computation.28 | convolution fusion | flops 629145600 | bytes 8257536 | tf_op jit(solution)/shard_map/rab,cka->rckb/dot_general | solution.py:41
  130.1 1.5 multiply_add_fusion
  131.6 5.7 %fusion = f32[50,128,256]{2,1,0:T(8,128)S(1)} fusion(f32[256,256,1]{1,0,2:T(8,128)S(1)} %copy-done.6, f32[50,128,128]{1,2,0:T(8,128)S(1)} %get-tuple-element.13, f32[50,128,128]{1,2,0:T(8,128)S(1)} %get-tuple-element.12), kind=kOutput, calls=%fused_computation | convolution fusion | flops 2518220800 | bytes 13369344 | tf_op jit(solution)/shard_map/rkb,bm->rkm/dot_general | solution.py:47
  137.3 0.7 multiply_subtract_fusion.4
  139.0 3.5 %fusion.4 = f32[49,128,256]{2,1,0:T(8,128)S(1)} fusion(f32[256,256,1]{1,0,2:T(8,128)S(1)} %copy-done.18, f32[1,128,256]{2,1,0:T(8,128)S(1)} %bitcast.87, f32[16,128,128]{2,1,0:T(8,128)S(1)} %get-tuple-element.8, f32[16,128,128]{2,1,0:T(8,128)S(1)} %get-tuple-element.7, f32[16,128,128]{2,1,0:T(8,128)S(1)} %get-tuple-element.11, ...), kind=kOutput, calls=%fused_computation.4 | convolution fusion | flops 2475884544 | bytes 13107200 | tf_op jit(solution)/shard_map/rkb,bm->rkm/dot_general | solution.py:53
  142.5 1.0 subtract_bitcast_fusion
  143.5 2.3 fusion.18
  145.9 24.3 %all_to_all.22 = f32[4,16,49,128]{3,1,2,0:T(8,128)S(1)} all-to-all(f32[4,16,49,128]{3,1,2,0:T(8,128)S(1)} %bitcast.76), channel_id=1, replica_groups={{0,8,16,24},{32,40,48,56},{64,72,80,88},{96,104,112,120},{128,136,144,1..., dimensions={0} | all-to-all | bytes 3211264 | tf_op jit(solution)/shard_map/all_to_all | solution.py:76
  170.2 0.6 copy.42
  170.9 82.5 %all_to_all.23 = f32[16,4,49,128]{3,1,2,0:T(4,128)S(1)} all-to-all(f32[16,4,49,128]{3,1,2,0:T(4,128)S(1)} %copy.42), channel_id=1, replica_groups={{0,32,64,96,128,160,192,224,256,288,320,352,384,416,448,480},{8,40,72,1..., dimensions={0} | all-to-all | bytes 3211264 | tf_op jit(solution)/shard_map/all_to_all | solution.py:78
  253.4 2.7 collective-permute-start
  256.4 2.6 collective-permute-done
  259.0 2.7 %collective-permute-start.1 = (f32[4,128]{1,0:T(4,128)S(1)}, f32[4,128]{1,0:T(4,128)S(1)}, u32[]{:S(2)}, u32[]{:S(2)}) collective-permute-start(f32[4,128]{1,0:T(4,128)S(1)} %add.45), channel_id=1, source_target_pairs={{0,2},{1,3},{2,0},{3,1},{4,6},{5,7},{6,4},{7,5},{8,10},{9,11},{10,... | collective-permute-start | bytes 6152 | tf_op jit(solution)/shard_map/ppermute | solution.py:137
  261.7 1.4 fusion.25
  263.1 1.3 collective-permute-done.1
  264.5 3.3 %collective-permute-start.2 = (f32[4,128]{1,0:T(4,128)S(1)}, f32[4,128]{1,0:T(4,128)S(1)}, u32[]{:S(2)}, u32[]{:S(2)}) collective-permute-start(f32[4,128]{1,0:T(4,128)S(1)} %add.46), channel_id=1, source_target_pairs={{0,4},{1,5},{2,6},{3,7},{4,0},{5,1},{6,2},{7,3},{8,12},{9,13},{10,... | collective-permute-start | bytes 6152 | tf_op jit(solution)/shard_map/ppermute | solution.py:137
  267.8 0.9 multiply_convert_fusion
  268.7 2.7 collective-permute-done.2
  271.4 0.6 add.47
  (57 shorter events, 3.2 us)
Async XLA Ops:
  0.6 2.9 %copy-start.1 = (bf16[1024,128]{1,0:T(8,128)(2,1)S(1)}, bf16[1024,128]{1,0:T(8,128)(2,1)}, u32[]{:S(2)}) copy-start(bf16[1024,128]{1,0:T(8,128)(2,1)} %param.17) | copy-start | bytes 786436
  0.6 2.9 %copy-start = (bf16[1024,128]{1,0:T(8,128)(2,1)S(1)}, bf16[1024,128]{1,0:T(8,128)(2,1)}, u32[]{:S(2)}) copy-start(bf16[1024,128]{1,0:T(8,128)(2,1)} %param.27) | copy-start | bytes 786436
  0.7 3.3 %copy-start.17 = (f32[4,128]{1,0:T(4,128)S(1)}, f32[4,128]{1,0:T(4,128)}, u32[]{:S(2)}) copy-start(f32[4,128]{1,0:T(4,128)} %param.20) | copy-start | bytes 6148
  0.7 3.3 %copy-start.16 = (f32[4,128]{1,0:T(4,128)S(1)}, f32[4,128]{1,0:T(4,128)}, u32[]{:S(2)}) copy-start(f32[4,128]{1,0:T(4,128)} %param.25) | copy-start | bytes 6148
  31.9 95.4 %copy-start.11 = (f32[2,128,64,1]{1,2,0,3:T(8,128)S(1)}, f32[2,128,64,1]{1,2,0,3:T(8,128)}, u32[]{:S(2)}) copy-start(f32[2,128,64,1]{1,2,0,3:T(8,128)} %constant.21) | copy-start | bytes 196612
  127.3 2.8 %copy-start.12 = (f32[128,128]{0,1:T(8,128)S(1)}, f32[128,128]{0,1:T(8,128)}, u32[]{:S(2)}) copy-start(f32[128,128]{0,1:T(8,128)} %constant.18.clone) | copy-start | bytes 196612
  127.3 2.8 %copy-start.13 = (f32[128,128]{0,1:T(8,128)S(1)}, f32[128,128]{0,1:T(8,128)}, u32[]{:S(2)}) copy-start(f32[128,128]{0,1:T(8,128)} %constant.19.clone) | copy-start | bytes 196612
  130.1 1.5 copy-start.6
  138.0 1.0 copy-start.18
  138.9 3.5 %copy-start.9 = (f32[128,128]{1,0:T(8,128)S(1)}, f32[128,128]{1,0:T(8,128)}, u32[]{:S(2)}) copy-start(f32[128,128]{1,0:T(8,128)} %constant.24) | copy-start | bytes 196612
  139.0 3.5 %copy-start.10 = (f32[128,128]{1,0:T(8,128)S(1)}, f32[128,128]{1,0:T(8,128)}, u32[]{:S(2)}) copy-start(f32[128,128]{1,0:T(8,128)} %constant.25) | copy-start | bytes 196612
  142.5 1.0 copy-start.8
  253.3 8.4 %copy-start.2 = (bf16[1024,128]{1,0:T(8,128)(2,1)S(1)}, bf16[1024,128]{1,0:T(8,128)(2,1)}, u32[]{:S(2)}) copy-start(bf16[1024,128]{1,0:T(8,128)(2,1)} %param.19) | copy-start | bytes 786436
  253.3 8.4 %copy-start.3 = (bf16[1024,128]{1,0:T(8,128)(2,1)S(1)}, bf16[1024,128]{1,0:T(8,128)(2,1)}, u32[]{:S(2)}) copy-start(bf16[1024,128]{1,0:T(8,128)(2,1)} %param.18) | copy-start | bytes 786436
  253.3 8.4 %copy-start.14 = (f32[1024]{0:T(1024)S(1)}, f32[1024]{0:T(1024)}, u32[]{:S(2)}) copy-start(f32[1024]{0:T(1024)} %param.21) | copy-start | bytes 12292
  253.4 5.6 %collective-permute-start = (f32[4,128]{1,0:T(4,128)S(1)}, f32[4,128]{1,0:T(4,128)S(1)}, u32[]{:S(2)}, u32[]{:S(2)}) collective-permute-start(f32[4,128]{1,0:T(4,128)S(1)} %slice_reduce_fusion), channel_id=1, source_target_pairs={{0,1},{1,0},{2,3},{3,2},{4,5},{5,4},{6,7},{7,6},{8,9},{9,8},{10,11... | collective-permute-start | bytes 6152 | tf_op jit(solution)/shard_map/ppermute | solution.py:137
  256.3 11.5 %copy-start.4 = (bf16[1024,128]{1,0:T(8,128)(2,1)S(1)}, bf16[1024,128]{1,0:T(8,128)(2,1)}, u32[]{:S(2)}) copy-start(bf16[1024,128]{1,0:T(8,128)(2,1)} %param.24) | copy-start | bytes 786436
  256.3 11.5 %copy-start.5 = (bf16[1024,128]{1,0:T(8,128)(2,1)S(1)}, bf16[1024,128]{1,0:T(8,128)(2,1)}, u32[]{:S(2)}) copy-start(bf16[1024,128]{1,0:T(8,128)(2,1)} %param.23) | copy-start | bytes 786436
  256.3 11.5 %copy-start.7 = (bf16[1024,128]{1,0:T(8,128)(2,1)S(1)}, bf16[1024,128]{1,0:T(8,128)(2,1)}, u32[]{:S(2)}) copy-start(bf16[1024,128]{1,0:T(8,128)(2,1)} %param.22) | copy-start | bytes 786436
  256.3 11.5 %copy-start.15 = (f32[1024]{0:T(1024)S(1)}, f32[1024]{0:T(1024)}, u32[]{:S(2)}) copy-start(f32[1024]{0:T(1024)} %param.26) | copy-start | bytes 12292
  259.0 5.5 %collective-permute-start.1 = (f32[4,128]{1,0:T(4,128)S(1)}, f32[4,128]{1,0:T(4,128)S(1)}, u32[]{:S(2)}, u32[]{:S(2)}) collective-permute-start(f32[4,128]{1,0:T(4,128)S(1)} %add.45), channel_id=1, source_target_pairs={{0,2},{1,3},{2,0},{3,1},{4,6},{5,7},{6,4},{7,5},{8,10},{9,11},{10,... | collective-permute-start | bytes 6152 | tf_op jit(solution)/shard_map/ppermute | solution.py:137
  264.5 7.0 %collective-permute-start.2 = (f32[4,128]{1,0:T(4,128)S(1)}, f32[4,128]{1,0:T(4,128)S(1)}, u32[]{:S(2)}, u32[]{:S(2)}) collective-permute-start(f32[4,128]{1,0:T(4,128)S(1)} %add.46), channel_id=1, source_target_pairs={{0,4},{1,5},{2,6},{3,7},{4,0},{5,1},{6,2},{7,3},{8,12},{9,13},{10,... | collective-permute-start | bytes 6152 | tf_op jit(solution)/shard_map/ppermute | solution.py:137

commit v5 on v2

--- a/solution.py
+++ b/solution.py
@@ -110,12 +110,18 @@
     conv_ref = cmul(fspec[1], href, False, width)
     corr = cmul(fspec[2], hpol, True, width)
     cross = jnp.sum(cmul(fspec[2], fspec[0], True, width), axis=0, keepdims=True)
-    prods = jnp.concatenate([conv_pol, conv_ref, corr, cross], axis=0)
-    back = inverse_dft(prods, tab)
+    partial = inverse_dft(cross, tab)
+    chan_size = lax.axis_size("chan")
+    bit = 1
+    while bit < chan_size:
+        pairs = [(i, i ^ bit) for i in range(chan_size)]
+        partial = partial + lax.ppermute(partial, "chan", pairs)
+        bit *= 2
+    prods = jnp.concatenate([conv_pol, conv_ref, corr], axis=0)
+    back = jnp.concatenate([inverse_dft(prods, tab), partial], axis=0)
     returned = lax.all_to_all(back, "ctx", split_axis=1, concat_axis=0, tiled=True)
     returned = returned.reshape(blocks, group_count, 3 * own_rows + 1, span)
     grad_filter = jnp.sum(returned[:, :, 3 * own_rows], axis=0)
-    grad_filter = lax.psum(grad_filter, "chan")
     returned = returned[:, :, : 3 * own_rows].reshape(blocks, group_count, 3, own_rows, span)
     returned = returned.transpose(2, 0, 3, 1, 4).reshape(3, chan_rows, span)
 

time: 249 us -> 245 us (0.984); the launches traced: 245 us -> 244 us
  blocking collectives: 219 us -> 204 us
  starting transfers between devices: 0 us -> 8.95 us
  waiting for transfers between devices: 0 us -> 4.07 us
    psum x1 -> x0, blocking collectives: 16.1 us -> none  [local(): grad_filter = lax.psum(grad_filter, 'chan')]
    ppermute x0 -> x3, starting transfers between devices: none -> 8.95 us  [local(): partial = partial + lax.ppermute(partial, 'chan', pairs)]
    ppermute x0 -> x3, waiting for transfers between devices: none -> 4.07 us  [local(): partial = partial + lax.ppermute(partial, 'chan', pairs)]
  transfers between devices with their start and end apart: 0 -> 3, of which waited for: 0 -> 2; matrix products, arithmetic and copies ran while one was open for 0% -> 3% of each run, Pallas kernels for 0% -> 0%
where the time goes in v5:
time: 245 us; the launch traced here: 244 us
  blocking collectives  204 us (83%)
  matrix products  13.9 us (6%)
  other arithmetic  9.89 us (4%)
  starting transfers between devices  8.95 us (4%)
  waiting for transfers between devices  4.07 us (2%)
  local copies, waits for them, and re-layouts  2.71 us (1%)
    all_to_all x1, blocking collectives, local(): recv = lax.all_to_all(send, 'ctx', split_axis=0, concat_axis=1, tiled=True)  108 us
    all_to_all x1, blocking collectives, local(): lax.all_to_all(back, 'ctx', split_axis=1, concat_axis=0, tiled=True)  95.5 us
    ppermute x3, starting transfers between devices, local(): partial = partial + lax.ppermute(partial, 'chan', pairs)  8.95 us
    dot_general x1, matrix products, forward_dft(): return jnp.einsum('rkb,bm->rkm', z, tab['fwd_b'], precision=PREC)  5.66 us
  transfers between devices with their start and end apart: 3, of which 2 were waited for; matrix products, arithmetic and copies ran while one was open for 3% of the time, Pallas kernels for 0%

profile of v5, /device:TPU:6, one launch (start us, length us, event | category | flops | bytes accessed | tf_op | source)
XLA Modules:
  0.0 244.5 jit_solution(10220359258583683670)
XLA Ops:
  0.7 0.8 pad_maximum_fusion.3
  1.4 1.1 convert_multiply_fusion.1
  2.5 1.1 convert_multiply_fusion.6
  4.1 108.4 %all_to_all.26 = f32[64,50,128]{2,1,0:T(8,128)S(1)} all-to-all(f32[64,50,128]{2,1,0:T(8,128)S(1)} %pad_maximum_fusion), channel_id=1, replica_groups=mesh['ctx'=64,'chan'=8] {'ctx'}, dimensions={0} | all-to-all | bytes 3276800 | tf_op jit(solution)/shard_map/all_to_all | solution.py:99
  112.5 2.8 %convolution_bitcast_fusion = f32[50,2,128,128]{2,3,1,0:T(8,128)S(1)} fusion(f32[2,128,64,1]{1,2,0,3:T(8,128)S(1)} %copy-done.12, f32[64,50,128]{2,1,0:T(8,128)S(1)} %all_to_all.26), kind=kOutput, calls=%fused_computation.26 | convolution fusion | flops 629145600 | bytes 8257536 | tf_op jit(solution)/shard_map/rab,cka->rckb/dot_general | solution.py:40
  115.3 1.5 multiply_add_fusion
  116.8 5.7 %fusion = f32[50,128,256]{2,1,0:T(8,128)S(1)} fusion(f32[256,256,1]{1,0,2:T(8,128)S(1)} %copy-done.6, f32[50,128,128]{1,2,0:T(8,128)S(1)} %get-tuple-element.13, f32[50,128,128]{1,2,0:T(8,128)S(1)} %get-tuple-element.12), kind=kOutput, calls=%fused_computation | convolution fusion | flops 2518220800 | bytes 13369344 | tf_op jit(solution)/shard_map/rkb,bm->rkm/dot_general | solution.py:46
  122.5 0.7 multiply_subtract_fusion.4
  123.7 0.4 copy-done.15
  124.3 2.8 %collective-permute-start = (f32[1,8192]{1,0:T(1,128)S(1)}, f32[1,8192]{1,0:T(1,128)S(1)}, u32[]{:S(2)}, u32[]{:S(2)}) collective-permute-start(f32[1,8192]{1,0:T(1,128)S(1)} %bitcast.97), channel_id=1, source_target_pairs={{0,1},{1,0},{2,3},{3,2},{4,5},{5,4},{6,7},{7,6},{8,9},{9,8},{10,11... | collective-permute-start | bytes 98312 | tf_op jit(solution)/shard_map/ppermute | solution.py:118
  127.1 0.3 multiply_subtract_fusion.3
  127.4 3.0 %fusion.4 = f32[48,128,256]{2,1,0:T(8,128)S(1)} fusion(f32[256,256,1]{1,0,2:T(8,128)S(1)} %copy-done.20, f32[16,128,128]{2,1,0:T(8,128)S(1)} %get-tuple-element.8, f32[16,128,128]{2,1,0:T(8,128)S(1)} %get-tuple-element.7, f32[16,128,128]{2,1,0:T(8,128)S(1)} %get-tuple-element.11, f32[16,128,128]{2,1,0:T(8,128)S(1)} %get-tuple-element.10, ...), kind=kOutput, calls=%fused_computation.4 | convolution fusion | flops 2423783424 | bytes 12845056 | tf_op jit(solution)/shard_map/rkb,bm->rkm/dot_general | solution.py:52
  130.5 2.9 %collective-permute-start.1 = (f32[1,8192]{1,0:T(1,128)S(1)}, f32[1,8192]{1,0:T(1,128)S(1)}, u32[]{:S(2)}, u32[]{:S(2)}) collective-permute-start(f32[1,8192]{1,0:T(1,128)S(1)} %add.46), channel_id=1, source_target_pairs={{0,2},{1,3},{2,0},{3,1},{4,6},{5,7},{6,4},{7,5},{8,10},{9,11},{10,... | collective-permute-start | bytes 98312 | tf_op jit(solution)/shard_map/ppermute | solution.py:118
  133.4 0.9 subtract_bitcast_fusion
  134.3 2.1 collective-permute-done.1
  136.5 3.3 %collective-permute-start.2 = (f32[1,8192]{1,0:T(1,128)S(1)}, f32[1,8192]{1,0:T(1,128)S(1)}, u32[]{:S(2)}, u32[]{:S(2)}) collective-permute-start(f32[1,8192]{1,0:T(1,128)S(1)} %add.47), channel_id=1, source_target_pairs={{0,4},{1,5},{2,6},{3,7},{4,0},{5,1},{6,2},{7,3},{8,12},{9,13},{10,... | collective-permute-start | bytes 98312 | tf_op jit(solution)/shard_map/ppermute | solution.py:118
  139.8 2.0 fusion.22
  141.8 2.0 collective-permute-done.2
  143.9 0.9 copy.42
  144.9 95.5 %all_to_all.27 = f32[49,64,128]{2,0,1:T(8,128)S(1)} all-to-all(f32[49,64,128]{2,0,1:T(8,128)S(1)} %copy.42), channel_id=1, replica_groups=mesh['ctx'=64,'chan'=8] {'ctx'}, dimensions={1} | all-to-all | bytes 3211264 | tf_op jit(solution)/shard_map/all_to_all | solution.py:122
  240.5 0.6 slice_reduce_fusion
  241.1 0.7 copy.54
  242.2 1.4 fusion.28
  243.6 0.9 multiply_convert_fusion
  (61 shorter events, 1.8 us)
Async XLA Ops:
  0.6 3.1 %copy-start.2 = (bf16[1024,128]{1,0:T(8,128)(2,1)S(1)}, bf16[1024,128]{1,0:T(8,128)(2,1)}, u32[]{:S(2)}) copy-start(bf16[1024,128]{1,0:T(8,128)(2,1)} %param.19) | copy-start | bytes 786436
  0.6 3.1 %copy-start.3 = (bf16[1024,128]{1,0:T(8,128)(2,1)S(1)}, bf16[1024,128]{1,0:T(8,128)(2,1)}, u32[]{:S(2)}) copy-start(bf16[1024,128]{1,0:T(8,128)(2,1)} %param.18) | copy-start | bytes 786436
  3.9 108.5 %copy-start.12 = (f32[2,128,64,1]{1,2,0,3:T(8,128)S(1)}, f32[2,128,64,1]{1,2,0,3:T(8,128)}, u32[]{:S(2)}) copy-start(f32[2,128,64,1]{1,2,0,3:T(8,128)} %constant.22) | copy-start | bytes 196612
  112.5 2.8 %copy-start.13 = (f32[128,128]{0,1:T(8,128)S(1)}, f32[128,128]{0,1:T(8,128)}, u32[]{:S(2)}) copy-start(f32[128,128]{0,1:T(8,128)} %constant.19.clone) | copy-start | bytes 196612
  112.5 2.8 %copy-start.14 = (f32[128,128]{0,1:T(8,128)S(1)}, f32[128,128]{0,1:T(8,128)}, u32[]{:S(2)}) copy-start(f32[128,128]{0,1:T(8,128)} %constant.18.clone) | copy-start | bytes 196612
  115.3 1.5 copy-start.6
  122.5 1.0 copy-start.7
  122.5 1.2 copy-start.16
  122.5 1.2 copy-start.17
  123.2 0.9 copy-start.15
  123.4 3.9 %copy-start.20 = (f32[256,256,1]{1,0,2:T(8,128)S(1)}, f32[256,256,1]{1,0,2:T(8,128)}, u32[]{:S(2)}) copy-start(f32[256,256,1]{1,0,2:T(8,128)} %constant.24) | copy-start | bytes 786436
  124.3 6.1 %collective-permute-start = (f32[1,8192]{1,0:T(1,128)S(1)}, f32[1,8192]{1,0:T(1,128)S(1)}, u32[]{:S(2)}, u32[]{:S(2)}) collective-permute-start(f32[1,8192]{1,0:T(1,128)S(1)} %bitcast.97), channel_id=1, source_target_pairs={{0,1},{1,0},{2,3},{3,2},{4,5},{5,4},{6,7},{7,6},{8,9},{9,8},{10,11... | collective-permute-start | bytes 98312 | tf_op jit(solution)/shard_map/ppermute | solution.py:118
  127.4 6.0 %copy-start.10 = (f32[128,128]{1,0:T(8,128)S(1)}, f32[128,128]{1,0:T(8,128)}, u32[]{:S(2)}) copy-start(f32[128,128]{1,0:T(8,128)} %constant.26) | copy-start | bytes 196612
  127.4 6.0 %copy-start.11 = (f32[128,128]{1,0:T(8,128)S(1)}, f32[128,128]{1,0:T(8,128)}, u32[]{:S(2)}) copy-start(f32[128,128]{1,0:T(8,128)} %constant.25) | copy-start | bytes 196612
  130.5 9.3 %copy-start.9 = (f32[2,128,64,1]{1,2,3,0:T(8,128)S(1)}, f32[2,128,64,1]{1,2,3,0:T(8,128)}, u32[]{:S(2)}) copy-start(f32[2,128,64,1]{1,2,3,0:T(8,128)} %constant.27) | copy-start | bytes 196612
  130.5 5.9 %collective-permute-start.1 = (f32[1,8192]{1,0:T(1,128)S(1)}, f32[1,8192]{1,0:T(1,128)S(1)}, u32[]{:S(2)}, u32[]{:S(2)}) collective-permute-start(f32[1,8192]{1,0:T(1,128)S(1)} %add.46), channel_id=1, source_target_pairs={{0,2},{1,3},{2,0},{3,1},{4,6},{5,7},{6,4},{7,5},{8,10},{9,11},{10,... | collective-permute-start | bytes 98312 | tf_op jit(solution)/shard_map/ppermute | solution.py:118
  136.5 7.3 %collective-permute-start.2 = (f32[1,8192]{1,0:T(1,128)S(1)}, f32[1,8192]{1,0:T(1,128)S(1)}, u32[]{:S(2)}, u32[]{:S(2)}) collective-permute-start(f32[1,8192]{1,0:T(1,128)S(1)} %add.47), channel_id=1, source_target_pairs={{0,4},{1,5},{2,6},{3,7},{4,0},{5,1},{6,2},{7,3},{8,12},{9,13},{10,... | collective-permute-start | bytes 98312 | tf_op jit(solution)/shard_map/ppermute | solution.py:118
  241.1 0.9 copy-start
  241.1 1.0 copy-start.1
  241.1 1.0 copy-start.18
  241.8 1.7 copy-start.4
  241.8 1.7 copy-start.5
  241.9 1.7 copy-start.8
  241.9 1.7 copy-start.19

commit v6 on v5

--- a/solution.py
+++ b/solution.py
@@ -95,8 +95,10 @@
     filt_rows = filt.shape[1]
     filt = jnp.broadcast_to(filt[None], (blocks, group_count, filt_rows, span))
     send = jnp.concatenate([fields, filt.reshape(shards, filt_rows, span)], axis=1)
-    send = send.reshape(shards * (3 * own_rows + filt_rows), span)
-    recv = lax.all_to_all(send, "ctx", split_axis=0, concat_axis=1, tiled=True)
+    rows_in = 3 * own_rows + filt_rows
+    send = send.reshape(shards, 1, rows_in * span)
+    recv = lax.all_to_all(send, "ctx", split_axis=0, concat_axis=0, tiled=True)
+    recv = recv.reshape(shards, rows_in, span).transpose(1, 0, 2).reshape(rows_in, shards * span)
     length = recv.shape[1]
     tab = dft_tables(length)
     width = tab["width"]
@@ -119,7 +121,9 @@
         bit *= 2
     prods = jnp.concatenate([conv_pol, conv_ref, corr], axis=0)
     back = jnp.concatenate([inverse_dft(prods, tab), partial], axis=0)
-    returned = lax.all_to_all(back, "ctx", split_axis=1, concat_axis=0, tiled=True)
+    rows_out = back.shape[0]
+    back = back.reshape(rows_out, shards, span).transpose(1, 0, 2).reshape(shards, 1, rows_out * span)
+    returned = lax.all_to_all(back, "ctx", split_axis=0, concat_axis=0, tiled=True)
     returned = returned.reshape(blocks, group_count, 3 * own_rows + 1, span)
     grad_filter = jnp.sum(returned[:, :, 3 * own_rows], axis=0)
     returned = returned[:, :, : 3 * own_rows].reshape(blocks, group_count, 3, own_rows, span)

time: 245 us -> 240 us (0.980)
  blocking collectives: 204 us -> 186 us
  other arithmetic: 9.89 us -> 19.2 us
  local copies, waits for them, and re-layouts: 2.71 us -> 6.27 us
    all_to_all x2, blocking collectives: 204 us -> 186 us  [the longest x1 100 us: local(): recv = lax.all_to_all(send, 'ctx', split_axis=0, concat_axis=0, tiled=True)]
    all_to_all x0 -> x2, other arithmetic: none -> 7.71 us  [the longest x1 3.9 us: local(): recv = lax.all_to_all(send, 'ctx', split_axis=0, concat_axis=0, tiled=True)]
    reshape x1 -> x3, local copies, waits for them, and re-layouts: 0.69 us -> 3.4 us  [the longest x1 1.59 us: local(): send = send.reshape(shards, 1, rows_in * span)]
where the time goes in v6:
time: 240 us; the launch traced here: 239 us
  blocking collectives  186 us (78%)
  other arithmetic  19.2 us (8%)
  matrix products  14.1 us (6%)
  starting transfers between devices  8.78 us (4%)
  local copies, waits for them, and re-layouts  6.27 us (3%)
  waiting for transfers between devices  4.06 us (2%)
    all_to_all x1, blocking collectives, local(): recv = lax.all_to_all(send, 'ctx', split_axis=0, concat_axis=0, tiled=True)  100 us
    all_to_all x1, blocking collectives, local(): lax.all_to_all(back, 'ctx', split_axis=0, concat_axis=0, tiled=True)  85.7 us
    ppermute x3, starting transfers between devices, local(): partial = partial + lax.ppermute(partial, 'chan', pairs)  8.78 us
    dot_general x1, matrix products, forward_dft(): return jnp.einsum('rkb,bm->rkm', z, tab['fwd_b'], precision=PREC)  5.88 us
  transfers between devices with their start and end apart: 3, of which 2 were waited for; matrix products, arithmetic and copies ran while one was open for 3% of the time, Pallas kernels for 0%

profile of v6, /device:TPU:6, one launch (start us, length us, event | category | flops | bytes accessed | tf_op | source)
XLA Modules:
  0.0 239.2 jit_solution(17787588363288183024)
XLA Ops:
  1.3 1.1 convert_multiply_fusion.1
  2.4 1.1 convert_multiply_fusion.6
  3.5 1.1 convert_multiply_fusion.3
  4.6 0.7 maximum_bitcast_fusion.1
  5.6 1.6 reshape.87
  7.2 100.1 %all_to_all.10 = f32[64,1,6400]{2,1,0:T(1,128)S(1)} all-to-all(f32[64,1,6400]{2,1,0:T(1,128)S(1)} %reshape.87), channel_id=1, replica_groups=mesh['ctx'=64,'chan'=8] {'ctx'}, dimensions={0} | all-to-all | bytes 3276800 | tf_op jit(solution)/shard_map/all_to_all | solution.py:100
  107.3 3.9 %reduce.1 = f32[64,6400]{1,0:T(8,128)S(1)} reduce(f32[64,1,6400]{2,1,0:T(1,128)S(1)} %all_to_all.10, f32[]{:T(128)} %constant.28), dimensions={1}, to_apply=%all_to_all.6.reduce_sub_computation | reduce | bytes 3276804 | tf_op jit(solution)/shard_map/all_to_all | solution.py:100
  111.2 2.8 %convolution_bitcast_fusion = f32[50,2,128,128]{2,3,1,0:T(8,128)S(1)} fusion(f32[2,128,64,1]{1,2,0,3:T(8,128)S(1)} %copy-done.14, f32[64,6400]{1,0:T(8,128)S(1)} %reduce.1), kind=kOutput, calls=%fused_computation.26 | convolution fusion | flops 629145600 | bytes 8257536 | tf_op jit(solution)/shard_map/rab,cka->rckb/dot_general | solution.py:40
  114.0 1.5 multiply_add_fusion
  115.5 5.9 %fusion = f32[50,128,256]{2,1,0:T(8,128)S(1)} fusion(f32[256,256,1]{1,0,2:T(8,128)S(1)} %copy-done.6, f32[50,128,128]{1,2,0:T(8,128)S(1)} %get-tuple-element.13, f32[50,128,128]{1,2,0:T(8,128)S(1)} %get-tuple-element.12), kind=kOutput, calls=%fused_computation | convolution fusion | flops 2518220800 | bytes 13369344 | tf_op jit(solution)/shard_map/rkb,bm->rkm/dot_general | solution.py:46
  123.2 2.6 %collective-permute-start = (f32[1,8192]{1,0:T(1,128)S(1)}, f32[1,8192]{1,0:T(1,128)S(1)}, u32[]{:S(2)}, u32[]{:S(2)}) collective-permute-start(f32[1,8192]{1,0:T(1,128)S(1)} %bitcast.99), channel_id=1, source_target_pairs={{0,1},{1,0},{2,3},{3,2},{4,5},{5,4},{6,7},{7,6},{8,9},{9,8},{10,11... | collective-permute-start | bytes 98312 | tf_op jit(solution)/shard_map/ppermute | solution.py:120
  126.2 3.0 %fusion.4 = f32[48,128,256]{2,1,0:T(8,128)S(1)} fusion(f32[256,256,1]{1,0,2:T(8,128)S(1)} %copy-done.20, f32[16,128,128]{2,1,0:T(8,128)S(1)} %get-tuple-element.8, f32[16,128,128]{2,1,0:T(8,128)S(1)} %get-tuple-element.7, f32[16,128,128]{2,1,0:T(8,128)S(1)} %get-tuple-element.11, f32[16,128,128]{2,1,0:T(8,128)S(1)} %get-tuple-element.10, ...), kind=kOutput, calls=%fused_computation.4 | convolution fusion | flops 2423783424 | bytes 12845056 | tf_op jit(solution)/shard_map/rkb,bm->rkm/dot_general | solution.py:52
  129.3 2.9 %collective-permute-start.1 = (f32[1,8192]{1,0:T(1,128)S(1)}, f32[1,8192]{1,0:T(1,128)S(1)}, u32[]{:S(2)}, u32[]{:S(2)}) collective-permute-start(f32[1,8192]{1,0:T(1,128)S(1)} %add.46), channel_id=1, source_target_pairs={{0,2},{1,3},{2,0},{3,1},{4,6},{5,7},{6,4},{7,5},{8,10},{9,11},{10,... | collective-permute-start | bytes 98312 | tf_op jit(solution)/shard_map/ppermute | solution.py:120
  132.2 0.9 subtract_bitcast_fusion
  133.1 2.1 collective-permute-done.1
  135.2 3.3 %collective-permute-start.2 = (f32[1,8192]{1,0:T(1,128)S(1)}, f32[1,8192]{1,0:T(1,128)S(1)}, u32[]{:S(2)}, u32[]{:S(2)}) collective-permute-start(f32[1,8192]{1,0:T(1,128)S(1)} %add.47), channel_id=1, source_target_pairs={{0,4},{1,5},{2,6},{3,7},{4,0},{5,1},{6,2},{7,3},{8,12},{9,13},{10,... | collective-permute-start | bytes 98312 | tf_op jit(solution)/shard_map/ppermute | solution.py:120
  138.6 2.0 fusion.21
  140.6 2.0 collective-permute-done.2
  142.7 0.9 copy.56
  143.7 1.6 reshape.88
  145.2 85.7 %all_to_all.11 = f32[64,1,6272]{2,1,0:T(1,128)S(1)} all-to-all(f32[64,1,6272]{2,1,0:T(1,128)S(1)} %reshape.88), channel_id=1, replica_groups=mesh['ctx'=64,'chan'=8] {'ctx'}, dimensions={0} | all-to-all | bytes 3211264 | tf_op jit(solution)/shard_map/all_to_all | solution.py:126
  230.9 3.8 %reduce.2 = f32[64,6272]{1,0:T(8,128)S(1)} reduce(f32[64,1,6272]{2,1,0:T(1,128)S(1)} %all_to_all.11, f32[]{:T(128)} %constant.28), dimensions={1}, to_apply=%all_to_all.7.reduce_sub_computation | reduce | bytes 3211268 | tf_op jit(solution)/shard_map/all_to_all | solution.py:126
  236.9 1.4 fusion.27
  238.3 0.9 multiply_convert_fusion
  (66 shorter events, 5.4 us)
Async XLA Ops:
  7.2 104.0 %copy-start.14 = (f32[2,128,64,1]{1,2,0,3:T(8,128)S(1)}, f32[2,128,64,1]{1,2,0,3:T(8,128)}, u32[]{:S(2)}) copy-start(f32[2,128,64,1]{1,2,0,3:T(8,128)} %constant.22) | copy-start | bytes 196612
  111.2 2.8 %copy-start.12 = (f32[128,128]{0,1:T(8,128)S(1)}, f32[128,128]{0,1:T(8,128)}, u32[]{:S(2)}) copy-start(f32[128,128]{0,1:T(8,128)} %constant.19.clone) | copy-start | bytes 196612
  111.2 2.8 %copy-start.13 = (f32[128,128]{0,1:T(8,128)S(1)}, f32[128,128]{0,1:T(8,128)}, u32[]{:S(2)}) copy-start(f32[128,128]{0,1:T(8,128)} %constant.18.clone) | copy-start | bytes 196612
  114.0 1.5 copy-start.6
  121.4 1.0 copy-start.7
  121.4 1.2 copy-start.16
  121.4 1.2 copy-start.17
  122.2 0.9 copy-start.15
  122.4 3.8 %copy-start.20 = (f32[256,256,1]{1,0,2:T(8,128)S(1)}, f32[256,256,1]{1,0,2:T(8,128)}, u32[]{:S(2)}) copy-start(f32[256,256,1]{1,0,2:T(8,128)} %constant.24) | copy-start | bytes 786436
  123.2 6.0 %collective-permute-start = (f32[1,8192]{1,0:T(1,128)S(1)}, f32[1,8192]{1,0:T(1,128)S(1)}, u32[]{:S(2)}, u32[]{:S(2)}) collective-permute-start(f32[1,8192]{1,0:T(1,128)S(1)} %bitcast.99), channel_id=1, source_target_pairs={{0,1},{1,0},{2,3},{3,2},{4,5},{5,4},{6,7},{7,6},{8,9},{9,8},{10,11... | collective-permute-start | bytes 98312 | tf_op jit(solution)/shard_map/ppermute | solution.py:120
  126.1 6.0 %copy-start.10 = (f32[128,128]{1,0:T(8,128)S(1)}, f32[128,128]{1,0:T(8,128)}, u32[]{:S(2)}) copy-start(f32[128,128]{1,0:T(8,128)} %constant.26) | copy-start | bytes 196612
  126.2 6.0 %copy-start.11 = (f32[128,128]{1,0:T(8,128)S(1)}, f32[128,128]{1,0:T(8,128)}, u32[]{:S(2)}) copy-start(f32[128,128]{1,0:T(8,128)} %constant.25) | copy-start | bytes 196612
  129.2 9.3 %copy-start.9 = (f32[2,128,64,1]{1,2,3,0:T(8,128)S(1)}, f32[2,128,64,1]{1,2,3,0:T(8,128)}, u32[]{:S(2)}) copy-start(f32[2,128,64,1]{1,2,3,0:T(8,128)} %constant.27) | copy-start | bytes 196612
  129.3 5.9 %collective-permute-start.1 = (f32[1,8192]{1,0:T(1,128)S(1)}, f32[1,8192]{1,0:T(1,128)S(1)}, u32[]{:S(2)}, u32[]{:S(2)}) collective-permute-start(f32[1,8192]{1,0:T(1,128)S(1)} %add.46), channel_id=1, source_target_pairs={{0,2},{1,3},{2,0},{3,1},{4,6},{5,7},{6,4},{7,5},{8,10},{9,11},{10,... | collective-permute-start | bytes 98312 | tf_op jit(solution)/shard_map/ppermute | solution.py:120
  135.2 7.3 %collective-permute-start.2 = (f32[1,8192]{1,0:T(1,128)S(1)}, f32[1,8192]{1,0:T(1,128)S(1)}, u32[]{:S(2)}, u32[]{:S(2)}) collective-permute-start(f32[1,8192]{1,0:T(1,128)S(1)} %add.47), channel_id=1, source_target_pairs={{0,4},{1,5},{2,6},{3,7},{4,0},{5,1},{6,2},{7,3},{8,12},{9,13},{10,... | collective-permute-start | bytes 98312 | tf_op jit(solution)/shard_map/ppermute | solution.py:120
  235.7 0.9 copy-start
  235.7 1.0 copy-start.1
  235.7 1.1 copy-start.2
  235.7 1.2 copy-start.3
  235.7 1.2 copy-start.18
  235.9 2.4 %copy-start.4 = (bf16[1024,128]{1,0:T(8,128)(2,1)S(1)}, bf16[1024,128]{1,0:T(8,128)(2,1)}, u32[]{:S(2)}) copy-start(bf16[1024,128]{1,0:T(8,128)(2,1)} %param.24) | copy-start | bytes 786436
  235.9 2.4 copy-start.5
  235.9 2.4 copy-start.8
  235.9 2.4 copy-start.19

commit v7 on v6

--- a/solution.py
+++ b/solution.py
@@ -114,11 +114,14 @@
     cross = jnp.sum(cmul(fspec[2], fspec[0], True, width), axis=0, keepdims=True)
     partial = inverse_dft(cross, tab)
     chan_size = lax.axis_size("chan")
-    bit = 1
-    while bit < chan_size:
-        pairs = [(i, i ^ bit) for i in range(chan_size)]
-        partial = partial + lax.ppermute(partial, "chan", pairs)
-        bit *= 2
+    shifted = [partial] + [
+        lax.ppermute(partial, "chan", [(i, (i + k) % chan_size) for i in range(chan_size)])
+        for k in range(1, chan_size)
+    ]
+    shifted = jnp.stack(shifted)
+    me = lax.axis_index("chan")
+    order = (me - jnp.arange(chan_size, dtype=jnp.int32)) % chan_size
+    partial = jnp.sum(jnp.take(shifted, order, axis=0), axis=0)
     prods = jnp.concatenate([conv_pol, conv_ref, corr], axis=0)
     back = jnp.concatenate([inverse_dft(prods, tab), partial], axis=0)
     rows_out = back.shape[0]

time: 240 us -> 255 us (1.062)
  blocking collectives: 186 us -> 85.6 us
  waiting for transfers between devices: 4.06 us -> 81.2 us
  starting transfers between devices: 8.78 us -> 42.3 us
    all_to_all x1 -> x0, blocking collectives: 100 us -> none  [local(): recv = lax.all_to_all(send, 'ctx', split_axis=0, concat_axis=0, tiled=True)]
    all_to_all x0 -> x1, waiting for transfers between devices: none -> 81.2 us  [local(): recv = lax.all_to_all(send, 'ctx', split_axis=0, concat_axis=0, tiled=True)]
    all_to_all x0 -> x1, starting transfers between devices: none -> 19 us  [local(): recv = lax.all_to_all(send, 'ctx', split_axis=0, concat_axis=0, tiled=True)]
    ppermute x3 -> x7, starting transfers between devices: 8.78 us -> 23.3 us  [local(): lax.ppermute(partial, 'chan', [(i, (i + k) % chan_size) for i in range(ch...]
    ppermute x3 -> x7, waiting for transfers between devices: 4.06 us -> 0.02 us  [local(): lax.ppermute(partial, 'chan', [(i, (i + k) % chan_size) for i in range(ch...]
  transfers between devices with their start and end apart: 3 -> 8, of which waited for: 2 -> 1; matrix products, arithmetic and copies ran while one was open for 3% -> 2% of each run, Pallas kernels for 0% -> 0%
where the time goes in v7:
time: 255 us; the launch traced here: 252 us
  blocking collectives  85.6 us (34%)
  waiting for transfers between devices  81.2 us (32%)
  starting transfers between devices  42.3 us (17%)
  other arithmetic  19.2 us (8%)
  matrix products  14 us (5%)
  local copies, waits for them, and re-layouts  8.49 us (3%)
    all_to_all x1, blocking collectives, local(): lax.all_to_all(back, 'ctx', split_axis=0, concat_axis=0, tiled=True)  85.6 us
    all_to_all x1, waiting for transfers between devices, local(): recv = lax.all_to_all(send, 'ctx', split_axis=0, concat_axis=0, tiled=True)  81.2 us
    ppermute x7, starting transfers between devices, local(): lax.ppermute(partial, 'chan', [(i, (i + k) % chan_size) for i in range(ch...  23.3 us
    all_to_all x1, starting transfers between devices, local(): recv = lax.all_to_all(send, 'ctx', split_axis=0, concat_axis=0, tiled=True)  19 us
    dot_general x1, matrix products, forward_dft(): return jnp.einsum('rkb,bm->rkm', z, tab['fwd_b'], precision=PREC)  5.88 us
  transfers between devices with their start and end apart: 8, of which 1 were waited for; matrix products, arithmetic and copies ran while one was open for 2% of the time, Pallas kernels for 0%

profile of v7, /device:TPU:6, one launch (start us, length us, event | category | flops | bytes accessed | tf_op | source)
XLA Modules:
  0.0 252.1 jit_solution(7411493473348841977)
XLA Ops:
  1.3 1.1 convert_multiply_fusion.1
  2.4 1.1 convert_multiply_fusion.6
  3.5 1.1 convert_multiply_fusion.3
  5.6 2.8 %reshape.178 = f32[64,1,6400]{2,1,0:T(1,128)} reshape(f32[64,50,128]{2,1,0:T(8,128)S(1)} %pad_maximum_fusion) | data formatting | bytes 3276800 | tf_op jit(solution)/shard_map/reshape | solution.py:99
  8.4 19.0 %all-to-all-start = ((f32[64,1,6400]{2,1,0:T(1,128)}), f32[64,1,6400]{2,1,0:T(1,128)S(1)}, u32[]{:S(2)}, u32[]{:S(2)}) async-start(f32[64,1,6400]{2,1,0:T(1,128)} %reshape.178), calls=%async_computation | async-start | bytes 3276800 | tf_op jit(solution)/shard_map/all_to_all | solution.py:100
  27.5 81.2 %all-to-all-done = f32[64,1,6400]{2,1,0:T(1,128)S(1)} async-done(((f32[64,1,6400]{2,1,0:T(1,128)}), f32[64,1,6400]{2,1,0:T(1,128)S(1)}, u32[]{:S(2)}, u32[]{:S(2)}) %all-to-all-start) | async-done | bytes 1638432 | tf_op jit(solution)/shard_map/all_to_all | solution.py:100
  108.7 3.9 %reduce.2 = f32[64,6400]{1,0:T(8,128)S(1)} reduce(f32[64,1,6400]{2,1,0:T(1,128)S(1)} %all-to-all-done, f32[]{:T(128)} %constant.62), dimensions={1}, to_apply=%all_to_all.6.reduce_sub_computation | reduce | bytes 3276804 | tf_op jit(solution)/shard_map/all_to_all | solution.py:100
  112.6 2.8 %convolution_bitcast_fusion = f32[50,2,128,128]{2,3,1,0:T(8,128)S(1)} fusion(f32[2,128,64,1]{1,2,0,3:T(8,128)S(1)} %copy-done.14, f32[64,6400]{1,0:T(8,128)S(1)} %reduce.2), kind=kOutput, calls=%fused_computation.27 | convolution fusion | flops 629145600 | bytes 8257536 | tf_op jit(solution)/shard_map/rab,cka->rckb/dot_general | solution.py:40
  115.4 1.5 multiply_add_fusion
  116.9 5.9 %fusion = f32[50,128,256]{2,1,0:T(8,128)S(1)} fusion(f32[256,256,1]{1,0,2:T(8,128)S(1)} %copy-done.6, f32[50,128,128]{1,2,0:T(8,128)S(1)} %get-tuple-element.13, f32[50,128,128]{1,2,0:T(8,128)S(1)} %get-tuple-element.12), kind=kOutput, calls=%fused_computation.1 | convolution fusion | flops 2518220800 | bytes 13369344 | tf_op jit(solution)/shard_map/rkb,bm->rkm/dot_general | solution.py:46
  124.6 2.6 %collective-permute-start = (f32[1,8192]{1,0:T(1,128)S(1)}, f32[1,8192]{1,0:T(1,128)S(1)}, u32[]{:S(2)}, u32[]{:S(2)}) collective-permute-start(f32[1,8192]{1,0:T(1,128)S(1)} %bitcast.118), channel_id=1, source_target_pairs={{0,1},{1,2},{2,3},{3,4},{4,5},{5,6},{6,7},{7,0},{8,9},{9,10},{10,1... | collective-permute-start | bytes 98312 | tf_op jit(solution)/shard_map/ppermute | solution.py:118
  127.2 2.4 collective-permute-start.1
  129.6 5.1 %collective-permute-start.2 = (f32[1,8192]{1,0:T(1,128)S(1)}, f32[1,8192]{1,0:T(1,128)S(1)}, u32[]{:S(2)}, u32[]{:S(2)}) collective-permute-start(f32[1,8192]{1,0:T(1,128)S(1)} %bitcast.120), channel_id=1, source_target_pairs={{0,3},{1,4},{2,5},{3,6},{4,7},{5,0},{6,1},{7,2},{8,11},{9,12},{10,... | collective-permute-start | bytes 98312 | tf_op jit(solution)/shard_map/ppermute | solution.py:118
  134.7 3.0 %collective-permute-start.3 = (f32[1,8192]{1,0:T(1,128)S(1)}, f32[1,8192]{1,0:T(1,128)S(1)}, u32[]{:S(2)}, u32[]{:S(2)}) collective-permute-start(f32[1,8192]{1,0:T(1,128)S(1)} %bitcast.121), channel_id=1, source_target_pairs={{0,4},{1,5},{2,6},{3,7},{4,0},{5,1},{6,2},{7,3},{8,12},{9,13},{10,... | collective-permute-start | bytes 98312 | tf_op jit(solution)/shard_map/ppermute | solution.py:118
  137.8 4.4 %collective-permute-start.4 = (f32[1,8192]{1,0:T(1,128)S(1)}, f32[1,8192]{1,0:T(1,128)S(1)}, u32[]{:S(2)}, u32[]{:S(2)}) collective-permute-start(f32[1,8192]{1,0:T(1,128)S(1)} %bitcast.122), channel_id=1, source_target_pairs={{0,5},{1,6},{2,7},{3,0},{4,1},{5,2},{6,3},{7,4},{8,13},{9,14},{10,... | collective-permute-start | bytes 98312 | tf_op jit(solution)/shard_map/ppermute | solution.py:118
  142.5 3.0 %fusion.4 = f32[48,128,256]{2,1,0:T(8,128)S(1)} fusion(f32[256,256,1]{1,0,2:T(8,128)S(1)} %copy-done.20, f32[16,128,128]{2,1,0:T(8,128)S(1)} %get-tuple-element.8, f32[16,128,128]{2,1,0:T(8,128)S(1)} %get-tuple-element.7, f32[16,128,128]{2,1,0:T(8,128)S(1)} %get-tuple-element.11, f32[16,128,128]{2,1,0:T(8,128)S(1)} %get-tuple-element.10, ...), kind=kOutput, calls=%fused_computation.5 | convolution fusion | flops 2423783424 | bytes 12845056 | tf_op jit(solution)/shard_map/rkb,bm->rkm/dot_general | solution.py:52
  145.6 0.9 subtract_bitcast_fusion
  146.6 1.9 collective-permute-start.5
  148.5 3.8 %collective-permute-start.6 = (f32[1,8192]{1,0:T(1,128)S(1)}, f32[1,8192]{1,0:T(1,128)S(1)}, u32[]{:S(2)}, u32[]{:S(2)}) collective-permute-start(f32[1,8192]{1,0:T(1,128)S(1)} %bitcast.124), channel_id=1, source_target_pairs={{0,7},{1,0},{2,1},{3,2},{4,3},{5,4},{6,5},{7,6},{8,15},{9,8},{10,9... | collective-permute-start | bytes 98312 | tf_op jit(solution)/shard_map/ppermute | solution.py:118
  152.3 2.0 fusion.21
  156.6 1.6 reshape.179
  158.2 85.6 %all_to_all.10 = f32[64,1,6272]{2,1,0:T(1,128)S(1)} all-to-all(f32[64,1,6272]{2,1,0:T(1,128)S(1)} %reshape.179), channel_id=1, replica_groups=mesh['ctx'=64,'chan'=8] {'ctx'}, dimensions={0} | all-to-all | bytes 3211264 | tf_op jit(solution)/shard_map/all_to_all | solution.py:129
  243.8 3.8 %reduce.3 = f32[64,6272]{1,0:T(8,128)S(1)} reduce(f32[64,1,6272]{2,1,0:T(1,128)S(1)} %all_to_all.10, f32[]{:T(128)} %constant.62), dimensions={1}, to_apply=%all_to_all.7.reduce_sub_computation | reduce | bytes 3211268 | tf_op jit(solution)/shard_map/all_to_all | solution.py:129
  249.8 1.4 fusion.27
  (78 shorter events, 9.1 us)
Async XLA Ops:
  8.4 104.2 %copy-start.14 = (f32[2,128,64,1]{1,2,0,3:T(8,128)S(1)}, f32[2,128,64,1]{1,2,0,3:T(8,128)}, u32[]{:S(2)}) copy-start(f32[2,128,64,1]{1,2,0,3:T(8,128)} %constant.56) | copy-start | bytes 196612
  8.4 100.3 %all-to-all-start = ((f32[64,1,6400]{2,1,0:T(1,128)}), f32[64,1,6400]{2,1,0:T(1,128)S(1)}, u32[]{:S(2)}, u32[]{:S(2)}) async-start(f32[64,1,6400]{2,1,0:T(1,128)} %reshape.178), calls=%async_computation | async-start | bytes 3276800 | tf_op jit(solution)/shard_map/all_to_all | solution.py:100
  112.6 2.8 %copy-start.12 = (f32[128,128]{0,1:T(8,128)S(1)}, f32[128,128]{0,1:T(8,128)}, u32[]{:S(2)}) copy-start(f32[128,128]{0,1:T(8,128)} %constant.53.clone) | copy-start | bytes 196612
  112.6 2.8 %copy-start.13 = (f32[128,128]{0,1:T(8,128)S(1)}, f32[128,128]{0,1:T(8,128)}, u32[]{:S(2)}) copy-start(f32[128,128]{0,1:T(8,128)} %constant.52.clone) | copy-start | bytes 196612
  115.4 1.5 copy-start.6
  122.8 1.2 copy-start.16
  122.8 1.2 copy-start.17
  123.8 18.7 %copy-start.20 = (f32[256,256,1]{1,0,2:T(8,128)S(1)}, f32[256,256,1]{1,0,2:T(8,128)}, u32[]{:S(2)}) copy-start(f32[256,256,1]{1,0,2:T(8,128)} %constant.58) | copy-start | bytes 786436
  124.6 21.9 %collective-permute-start = (f32[1,8192]{1,0:T(1,128)S(1)}, f32[1,8192]{1,0:T(1,128)S(1)}, u32[]{:S(2)}, u32[]{:S(2)}) collective-permute-start(f32[1,8192]{1,0:T(1,128)S(1)} %bitcast.118), channel_id=1, source_target_pairs={{0,1},{1,2},{2,3},{3,4},{4,5},{5,6},{6,7},{7,0},{8,9},{9,10},{10,1... | collective-permute-start | bytes 98312 | tf_op jit(solution)/shard_map/ppermute | solution.py:118
  127.2 21.3 %collective-permute-start.1 = (f32[1,8192]{1,0:T(1,128)S(1)}, f32[1,8192]{1,0:T(1,128)S(1)}, u32[]{:S(2)}, u32[]{:S(2)}) collective-permute-start(f32[1,8192]{1,0:T(1,128)S(1)} %bitcast.119), channel_id=1, source_target_pairs={{0,2},{1,3},{2,4},{3,5},{4,6},{5,7},{6,0},{7,1},{8,10},{9,11},{10,... | collective-permute-start | bytes 98312 | tf_op jit(solution)/shard_map/ppermute | solution.py:118
  129.6 24.7 %collective-permute-start.2 = (f32[1,8192]{1,0:T(1,128)S(1)}, f32[1,8192]{1,0:T(1,128)S(1)}, u32[]{:S(2)}, u32[]{:S(2)}) collective-permute-start(f32[1,8192]{1,0:T(1,128)S(1)} %bitcast.120), channel_id=1, source_target_pairs={{0,3},{1,4},{2,5},{3,6},{4,7},{5,0},{6,1},{7,2},{8,11},{9,12},{10,... | collective-permute-start | bytes 98312 | tf_op jit(solution)/shard_map/ppermute | solution.py:118
  134.7 19.6 %collective-permute-start.3 = (f32[1,8192]{1,0:T(1,128)S(1)}, f32[1,8192]{1,0:T(1,128)S(1)}, u32[]{:S(2)}, u32[]{:S(2)}) collective-permute-start(f32[1,8192]{1,0:T(1,128)S(1)} %bitcast.121), channel_id=1, source_target_pairs={{0,4},{1,5},{2,6},{3,7},{4,0},{5,1},{6,2},{7,3},{8,12},{9,13},{10,... | collective-permute-start | bytes 98312 | tf_op jit(solution)/shard_map/ppermute | solution.py:118
  137.8 16.6 %collective-permute-start.4 = (f32[1,8192]{1,0:T(1,128)S(1)}, f32[1,8192]{1,0:T(1,128)S(1)}, u32[]{:S(2)}, u32[]{:S(2)}) collective-permute-start(f32[1,8192]{1,0:T(1,128)S(1)} %bitcast.122), channel_id=1, source_target_pairs={{0,5},{1,6},{2,7},{3,0},{4,1},{5,2},{6,3},{7,4},{8,13},{9,14},{10,... | collective-permute-start | bytes 98312 | tf_op jit(solution)/shard_map/ppermute | solution.py:118
  142.5 3.0 %copy-start.10 = (f32[128,128]{1,0:T(8,128)S(1)}, f32[128,128]{1,0:T(8,128)}, u32[]{:S(2)}) copy-start(f32[128,128]{1,0:T(8,128)} %constant.60) | copy-start | bytes 196612
  142.5 3.0 %copy-start.11 = (f32[128,128]{1,0:T(8,128)S(1)}, f32[128,128]{1,0:T(8,128)}, u32[]{:S(2)}) copy-start(f32[128,128]{1,0:T(8,128)} %constant.59) | copy-start | bytes 196612
  145.6 6.7 %copy-start.9 = (f32[2,128,64,1]{1,2,3,0:T(8,128)S(1)}, f32[2,128,64,1]{1,2,3,0:T(8,128)}, u32[]{:S(2)}) copy-start(f32[2,128,64,1]{1,2,3,0:T(8,128)} %constant.61) | copy-start | bytes 196612
  146.6 7.8 %collective-permute-start.5 = (f32[1,8192]{1,0:T(1,128)S(1)}, f32[1,8192]{1,0:T(1,128)S(1)}, u32[]{:S(2)}, u32[]{:S(2)}) collective-permute-start(f32[1,8192]{1,0:T(1,128)S(1)} %bitcast.123), channel_id=1, source_target_pairs={{0,6},{1,7},{2,0},{3,1},{4,2},{5,3},{6,4},{7,5},{8,14},{9,15},{10,... | collective-permute-start | bytes 98312 | tf_op jit(solution)/shard_map/ppermute | solution.py:118
  148.5 5.8 %collective-permute-start.6 = (f32[1,8192]{1,0:T(1,128)S(1)}, f32[1,8192]{1,0:T(1,128)S(1)}, u32[]{:S(2)}, u32[]{:S(2)}) collective-permute-start(f32[1,8192]{1,0:T(1,128)S(1)} %bitcast.124), channel_id=1, source_target_pairs={{0,7},{1,0},{2,1},{3,2},{4,3},{5,4},{6,5},{7,6},{8,15},{9,8},{10,9... | collective-permute-start | bytes 98312 | tf_op jit(solution)/shard_map/ppermute | solution.py:118
  248.6 1.2 copy-start.3
  248.6 1.2 copy-start.18
  248.8 2.4 copy-start.4
  248.8 2.4 copy-start.5
  248.8 2.4 copy-start.8
  248.8 2.4 copy-start.19
  (5 other events, 4.9 us)
